TPU v7x, 256 devices: a whole 4x4x8 slice. The times are simulated.
256 devices in a mesh: row: 32 (over z, x), col: 8 (over y, core).
Axes of the slice: x: 4, y: 4, z: 8, core: 2. Of those that a mesh axis runs over, the one named last changes fastest.
Arguments:
- tokens: bfloat16 [1024, 8192], P('row', 'col'), may hold values from -6 to 6
- cotangent: bfloat16 [1024, 8192], P('row', 'col'), may hold values from -6 to 6
- gate_weight: bfloat16 [8192, 16384], P('col', 'row'), may hold values from -0.125 to 0.125
- up_weight: bfloat16 [8192, 16384], P('col', 'row'), may hold values from -0.125 to 0.125
- down_weight: bfloat16 [16384, 8192], P('row', 'col'), may hold values from -0.078125 to 0.078125
- gate_mask: int32 [64, 128], P('col', 'row'), may hold values 0 or 1
- up_mask: int32 [64, 128], P('col', 'row'), may hold values 0 or 1
- down_mask: int32 [128, 64], P('row', 'col'), may hold values 0 or 1
Outputs:
- layer_out: bfloat16 [1024, 8192], P('row', 'col')
- grad_tokens: bfloat16 [1024, 8192], P('row', 'col')
- grad_gate_weight: float32 [8192, 16384], P('col', 'row')
- grad_up_weight: float32 [8192, 16384], P('col', 'row')
- grad_down_weight: float32 [16384, 8192], P('row', 'col')
All inputs are finite; a program needn't handle non-finite values. No bound on the sum of `gate_mask` or of `up_mask` or of `down_mask` on one device may be relied on, other than what follows from the above.
Results may differ from a plain program's by a relative error of at most 0.0049.
Values may be sent and summed in bfloat16 or wider, within the bound.
No kernel may reach another device: no remote copies, remote signals or barrier semaphores. Data moves between devices by JAX's collectives and lax.ppermute only.
A program may use at most 128 MiB of HBM per device.

v0:
```python
import jax
import jax.numpy as jnp
from jax import lax
from jax.sharding import PartitionSpec as P

BLOCK = 128


contract_inner = (((1,), (1,)), ((), ()))
contract_outer = (((0,), (0,)), ((), ()))


def apply_pattern(weight, pattern):
    row_blocks, col_blocks = pattern.shape
    block_scale = pattern.astype(weight.dtype)
    blocks = weight.reshape(row_blocks, BLOCK, col_blocks, BLOCK) * block_scale[:, None, :, None]
    return blocks.reshape(weight.shape)


def col_reduce(summands, finish):
    summed = lax.psum(summands, "col")
    return finish(summed)


def shards(tokens, cotangent, gate_weight, up_weight, down_weight, gate_mask, up_mask, down_mask):
    hidden_width = gate_weight.shape[1]
    gathered_tokens, gathered_grads = (
        lax.all_gather(tokens, "row", axis=0, tiled=True),
        lax.all_gather(cotangent, "row", axis=0, tiled=True),
    )
    joint_weight = jnp.concatenate(
        [apply_pattern(gate_weight, gate_mask), apply_pattern(up_weight, up_mask)], axis=1
    )
    masked_down = apply_pattern(down_weight, down_mask)
    joint_part = jnp.dot(gathered_tokens, joint_weight, preferred_element_type=jnp.float32)

    def activate(joint_pre):
        gate_pre = joint_pre[:, :hidden_width]
        up_pre = joint_pre[:, hidden_width:]
        hidden_rows = (gate_pre * jax.nn.sigmoid(gate_pre) * up_pre).astype(jnp.bfloat16)
        return (hidden_rows, joint_pre)

    hidden, joint_pre = col_reduce(joint_part, activate)
    hidden_part = lax.dot_general(
        gathered_grads, masked_down, contract_inner, preferred_element_type=jnp.float32
    )

    def derive(grad_hidden):
        gate_pre = joint_pre[:, :hidden_width]
        up_pre = joint_pre[:, hidden_width:]
        sigmoid_gate = jax.nn.sigmoid(gate_pre)
        silu_gate = gate_pre * sigmoid_gate
        grad_gate_pre = (
            grad_hidden * up_pre * sigmoid_gate * (1.0 + gate_pre * (1.0 - sigmoid_gate))
        )
        grad_up_pre = grad_hidden * silu_gate
        joint_rows = jnp.concatenate(
            [grad_gate_pre.astype(jnp.bfloat16), grad_up_pre.astype(jnp.bfloat16)], axis=1
        )
        return (joint_rows, grad_hidden)

    joint_grad, unused = col_reduce(hidden_part, derive)
    output_term = jnp.dot(hidden, masked_down, preferred_element_type=jnp.float32)
    token_term = lax.dot_general(
        joint_grad, joint_weight, contract_inner, preferred_element_type=jnp.float32
    )
    layer_out, grad_tokens = (
        lax.psum_scatter(output_term, "row", scatter_dimension=0, tiled=True),
        lax.psum_scatter(token_term, "row", scatter_dimension=0, tiled=True),
    )
    weight_grads = lax.dot_general(
        gathered_tokens, joint_grad, contract_outer, preferred_element_type=jnp.float32
    )
    grad_gate_weight = apply_pattern(weight_grads[:, :hidden_width], gate_mask)
    grad_up_weight = apply_pattern(weight_grads[:, hidden_width:], up_mask)
    grad_down_weight = apply_pattern(
        lax.dot_general(hidden, gathered_grads, contract_outer, preferred_element_type=jnp.float32),
        down_mask,
    )
    return (
        layer_out.astype(jnp.bfloat16),
        grad_tokens.astype(jnp.bfloat16),
        grad_gate_weight,
        grad_up_weight,
        grad_down_weight,
    )


def solution(mesh):
    in_specs = (
        P("row", "col"),
        P("row", "col"),
        P("col", "row"),
        P("col", "row"),
        P("row", "col"),
        P("col", "row"),
        P("col", "row"),
        P("row", "col"),
    )
    out_specs = (
        P("row", "col"),
        P("row", "col"),
        P("col", "row"),
        P("col", "row"),
        P("row", "col"),
    )
    return jax.shard_map(shards, mesh=mesh, in_specs=in_specs, out_specs=out_specs, check_vma=False)
```

profile of v0, /device:TPU:8, one launch (start us, length us, event | category | flops | bytes accessed | tf_op | source)
XLA Modules:
  0.0 727.5 jit_solution(3877633077299212398)
XLA Ops:
  7.2 0.7 all-gather.3.cloned.1.call-update
  8.0 0.7 all-gather.5.cloned.1.call-update
  8.7 0.8 fusion.8
  9.6 0.8 fusion.7
  10.4 0.8 fusion.6
  11.2 0.3 mul.88
  11.5 0.3 mul.91
  11.9 1.3 bitcast_multiply_fusion.4
  13.2 78.2 %all-gather.3.cloned.1.call-done = bf16[1024,1024]{1,0:T(8,128)(2,1)} async-done(((bf16[32,1024]{1,0:T(8,128)(2,1)}), bf16[1024,1024]{1,0:T(8,128)(2,1)}) %all-gather.3.cloned.1.call-update) | async-done | bytes 2097168 | tf_op jit(solution)/shard_map/all_gather | solution.py:28
  91.4 6.4 convolution_bitcast_fusion.1
  97.8 71.4 %all-gather.5.cloned.1.call-done = bf16[1024,1024]{1,0:T(8,128)(2,1)} async-done(((bf16[32,1024]{1,0:T(8,128)(2,1)}), bf16[1024,1024]{1,0:T(8,128)(2,1)}) %all-gather.5.cloned.1.call-update) | async-done | bytes 2097168 | tf_op jit(solution)/shard_map/all_gather | solution.py:29
  169.2 0.2 mul.96
  169.4 4.2 convolution_bitcast_fusion.2
  173.7 84.3 %all-reduce.3.cloned.1.call-done = (f32[1024,1024]{0,1:T(8,128)}, f32[1024,512]{0,1:T(8,128)}) async-done(((f32[1024,1024]{0,1:T(8,128)}, f32[1024,512]{0,1:T(8,128)}), (f32[1024,1024]{0,1:T(8,128)}, f32[1024,512]{0,1:T(8,128)})) %all-reduce.3.cloned.1.call-update) | async-done | bytes 6291472 | tf_op jit(solution)/shard_map/psum | solution.py:21
  258.0 4.4 multiply_convert_fusion.1
  262.4 1.0 copy-done.1
  263.4 0.3 copy-done.3
  263.7 4.4 fusion.1
  268.1 0.2 reduce-scatter.3.cloned.1.call-start
  268.3 3.3 fusion.2
  271.6 1.2 copy-done.2
  272.8 0.3 copy-done.4
  273.1 3.9 convolution_bitcast_fusion
  277.4 2.8 bitcast_multiply_fusion.1
  280.3 2.9 copy.15
  283.2 1.8 copy.16
  285.2 1.4 copy-done.10
  286.6 2.7 bitcast_multiply_fusion
  289.3 204.7 %reduce-scatter.5.cloned.1.call-done = f32[32,1024]{1,0:T(8,128)} async-done(((f32[1024,1024]{1,0:T(8,128)}), f32[32,1024]{1,0:T(8,128)}) %reduce-scatter.5.cloned.1.call-update) | async-done | bytes 131088 | tf_op jit(solution)/shard_map/reduce_scatter | solution.py:69
  494.0 1.5 convert_element_type.40
  495.5 223.9 %reduce-scatter.3.cloned.1.call-done = f32[32,1024]{1,0:T(8,128)} async-done(((f32[1024,1024]{1,0:T(8,128)}), f32[32,1024]{1,0:T(8,128)}) %reduce-scatter.3.cloned.1.call-update) | async-done | bytes 131088 | tf_op jit(solution)/shard_map/reduce_scatter | solution.py:68
  719.5 1.5 convert_element_type.37
  (29 shorter events, 1.0 us)
Async XLA Ops:
  7.2 4.7 copy-start.6
  7.2 4.7 copy-start.5
  7.2 84.2 %all-gather.3.cloned.1.call-start = ((), (), s32[]{:S(2)}) async-start(), calls=%async_computation.2 | async-start | bytes 2162688 | tf_op jit(solution)/shard_map/all_gather | solution.py:28
  7.9 161.2 %all-gather.5.cloned.1.call-start = ((), (), s32[]{:S(2)}) async-start(), calls=%async_computation.4 | async-start | bytes 2162688 | tf_op jit(solution)/shard_map/all_gather | solution.py:29
  8.7 249.3 %all-reduce.3.cloned.1.call-start = ((), (), s32[]{:S(2)}) async-start(), calls=%async_computation.6 | async-start | bytes 12582912 | tf_op jit(solution)/shard_map/psum | solution.py:21
  13.2 84.6 %copy-start.7 = (bf16[1024,512]{1,0:T(8,128)(2,1)}, bf16[1024,512]{1,0:T(8,128)(2,1)S(1)}, u32[]{:S(2)}) copy-start(bf16[1024,512]{1,0:T(8,128)(2,1)S(1)} %get-tuple-element.23) | copy-start | bytes 3145732
  91.4 78.0 %copy-start = (bf16[512,1024]{1,0:T(8,128)(2,1)S(1)}, bf16[512,1024]{1,0:T(8,128)(2,1)}, u32[]{:S(2)}) copy-start(bf16[512,1024]{1,0:T(8,128)(2,1)} %param.12) | copy-start | bytes 3145732
  173.6 320.4 %reduce-scatter.5.cloned.1.call-start = ((), (), s32[]{:S(2)}) async-start(), calls=%async_computation.5 | async-start | bytes 4325376 | tf_op jit(solution)/shard_map/reduce_scatter | solution.py:69
  258.0 5.7 copy-start.8
  258.0 5.7 copy-start.9
  262.3 1.0 copy-start.1
  262.4 1.3 copy-start.3
  268.1 451.4 %reduce-scatter.3.cloned.1.call-start = ((), (), s32[]{:S(2)}) async-start(), calls=%async_computation.3 | async-start | bytes 4325376 | tf_op jit(solution)/shard_map/reduce_scatter | solution.py:68
  271.6 1.2 copy-start.2
  271.6 1.5 copy-start.4
  285.0 1.6 copy-start.10
Sparse Core Ops, SparseCore 0:
  10.6 80.7 all-gather.2
  94.0 75.1 all-gather.4
  173.7 84.1 all-reduce.2
  268.2 225.7 reduce-scatter.4
  497.7 221.6 reduce-scatter.2
where the time goes:
time: 728 us
  waiting for transfers between devices  664 us (91%)
  matrix products  24.9 us (3%)
  other arithmetic  13.9 us (2%)
  between operations  13.9 us (2%)
  local copies, waits for them, and re-layouts  10.6 us (1%)
    reduce_scatter x1, waiting for transfers between devices, shards(): lax.psum_scatter(output_term, 'row', scatter_dimension=0, tiled=True)  224 us
    reduce_scatter x1, waiting for transfers between devices, shards(): lax.psum_scatter(token_term, 'row', scatter_dimension=0, tiled=True)  205 us
    psum x1, waiting for transfers between devices, col_reduce(): summed = lax.psum(summands, 'col')  84.3 us
    all_gather x1, waiting for transfers between devices, shards(): lax.all_gather(tokens, 'row', axis=0, tiled=True)  78.2 us
    all_gather x1, waiting for transfers between devices, shards(): lax.all_gather(cotangent, 'row', axis=0, tiled=True)  71.4 us
  transfers between devices with their start and end apart: 5, of which 5 were waited for; matrix products, arithmetic and copies ran while one was open for 4% of the time, Pallas kernels for 0%

commit v1 on v0

v1 whole, which is shorter than its diff:
```python
import jax
import jax.numpy as jnp
from jax import lax
from jax.sharding import PartitionSpec as P

BLOCK = 128


contract_inner = (((1,), (1,)), ((), ()))
contract_outer = (((0,), (0,)), ((), ()))


def apply_pattern(weight, pattern):
    row_blocks, col_blocks = pattern.shape
    block_scale = pattern.astype(weight.dtype)
    blocks = weight.reshape(row_blocks, BLOCK, col_blocks, BLOCK) * block_scale[:, None, :, None]
    return blocks.reshape(weight.shape)


def gather_rows(x, axis, n):
    tiled = jnp.tile(x, (n, 1))
    return lax.all_to_all(tiled, axis, 0, 0, tiled=True)


def reduce_rows(x, axis, n):
    got = lax.all_to_all(x, axis, 0, 0, tiled=True)
    rows = x.shape[0] // n
    return jnp.sum(got.reshape(n, rows, x.shape[1]), axis=0)


def shards(tokens, cotangent, gate_weight, up_weight, down_weight, gate_mask, up_mask, down_mask):
    n_row = lax.axis_size("row")
    n_col = lax.axis_size("col")
    hidden_width = gate_weight.shape[1]
    features = tokens.shape[1]
    both = gather_rows(jnp.concatenate([tokens, cotangent], axis=1), "row", n_row)
    gathered_tokens = both[:, :features]
    gathered_grads = both[:, features:]
    joint_weight = jnp.concatenate(
        [apply_pattern(gate_weight, gate_mask), apply_pattern(up_weight, up_mask)], axis=1
    )
    masked_down = apply_pattern(down_weight, down_mask)
    joint_part = jnp.dot(gathered_tokens, joint_weight, preferred_element_type=jnp.float32)
    hidden_part = lax.dot_general(
        gathered_grads, masked_down, contract_inner, preferred_element_type=jnp.float32
    )
    sums = reduce_rows(jnp.concatenate([joint_part, hidden_part], axis=1), "col", n_col)
    gate_pre = sums[:, :hidden_width]
    up_pre = sums[:, hidden_width:2 * hidden_width]
    grad_hidden = sums[:, 2 * hidden_width:]
    sigmoid_gate = jax.nn.sigmoid(gate_pre)
    silu_gate = gate_pre * sigmoid_gate
    hidden_rows = (silu_gate * up_pre).astype(jnp.bfloat16)
    grad_gate_pre = grad_hidden * up_pre * sigmoid_gate * (1.0 + gate_pre * (1.0 - sigmoid_gate))
    grad_up_pre = grad_hidden * silu_gate
    rows = jnp.concatenate(
        [hidden_rows, grad_gate_pre.astype(jnp.bfloat16), grad_up_pre.astype(jnp.bfloat16)], axis=1
    )
    full = gather_rows(rows, "col", n_col)
    hidden = full[:, :hidden_width]
    joint_grad = full[:, hidden_width:]
    output_term = jnp.dot(hidden, masked_down, preferred_element_type=jnp.float32)
    token_term = lax.dot_general(
        joint_grad, joint_weight, contract_inner, preferred_element_type=jnp.float32
    )
    outs = reduce_rows(jnp.concatenate([output_term, token_term], axis=1), "row", n_row)
    layer_out = outs[:, :features]
    grad_tokens = outs[:, features:]
    weight_grads = lax.dot_general(
        gathered_tokens, joint_grad, contract_outer, preferred_element_type=jnp.float32
    )
    grad_gate_weight = apply_pattern(weight_grads[:, :hidden_width], gate_mask)
    grad_up_weight = apply_pattern(weight_grads[:, hidden_width:], up_mask)
    grad_down_weight = apply_pattern(
        lax.dot_general(hidden, gathered_grads, contract_outer, preferred_element_type=jnp.float32),
        down_mask,
    )
    return (
        layer_out.astype(jnp.bfloat16),
        grad_tokens.astype(jnp.bfloat16),
        grad_gate_weight,
        grad_up_weight,
        grad_down_weight,
    )


def solution(mesh):
    in_specs = (
        P("row", "col"),
        P("row", "col"),
        P("col", "row"),
        P("col", "row"),
        P("row", "col"),
        P("col", "row"),
        P("col", "row"),
        P("row", "col"),
    )
    out_specs = (
        P("row", "col"),
        P("row", "col"),
        P("col", "row"),
        P("col", "row"),
        P("row", "col"),
    )
    return jax.shard_map(shards, mesh=mesh, in_specs=in_specs, out_specs=out_specs, check_vma=False)
```

time: 728 us -> 462 us (0.63)
  waiting for transfers between devices: 664 us -> 270 us
  blocking collectives: 0 us -> 117 us
  starting transfers between devices: 0.38 us -> 18.8 us
  between operations: 13.9 us -> 0.88 us
    reduce_scatter x2 -> x0, waiting for transfers between devices: 429 us -> none  [the longest x1 224 us: shards(): lax.psum_scatter(output_term, 'row', scatter_dimension=0, tiled=True)]
    all_to_all x0 -> x2, waiting for transfers between devices: none -> 270 us  [the longest x1 178 us: reduce_rows(): got = lax.all_to_all(x, axis, 0, 0, tiled=True)]
    all_gather x2 -> x0, waiting for transfers between devices: 150 us -> none  [the longest x1 78.2 us: shards(): lax.all_gather(tokens, 'row', axis=0, tiled=True)]
    all_to_all x0 -> x2, blocking collectives: none -> 117 us  [the longest x1 76.3 us: reduce_rows(): got = lax.all_to_all(x, axis, 0, 0, tiled=True)]
    psum x1 -> x0, waiting for transfers between devices: 84.3 us -> none  [col_reduce(): summed = lax.psum(summands, 'col')]
    all_to_all x0 -> x2, starting transfers between devices: none -> 18.8 us  [the longest x1 11.6 us: gather_rows(): return lax.all_to_all(tiled, axis, 0, 0, tiled=True)]
    concatenate x0 -> x2, local copies, waits for them, and re-layouts: none -> 9.37 us  [the longest x1 9.19 us: shards(): jnp.concatenate([output_term, token_term], axis=1)]
    unnamed x24, local copies, waits for them, and re-layouts: 8.91 us -> 1.01 us
  transfers between devices with their start and end apart: 5 -> 2, of which waited for: 5 -> 2; matrix products, arithmetic and copies ran while one was open for 4% -> 3% of each run, Pallas kernels for 0% -> 0%
where the time goes in v1:
time: 462 us; the launch traced here: 458 us
  waiting for transfers between devices  270 us (58%)
  blocking collectives  117 us (25%)
  matrix products  19.2 us (4%)
  starting transfers between devices  18.8 us (4%)
  other arithmetic  16.9 us (4%)
  local copies, waits for them, and re-layouts  15.9 us (3%)
    all_to_all x1, waiting for transfers between devices, reduce_rows(): got = lax.all_to_all(x, axis, 0, 0, tiled=True)  178 us
    all_to_all x1, waiting for transfers between devices, gather_rows(): return lax.all_to_all(tiled, axis, 0, 0, tiled=True)  92.1 us
    all_to_all x1, blocking collectives, reduce_rows(): got = lax.all_to_all(x, axis, 0, 0, tiled=True)  76.3 us
    all_to_all x1, blocking collectives, gather_rows(): return lax.all_to_all(tiled, axis, 0, 0, tiled=True)  40.6 us
    all_to_all x1, starting transfers between devices, gather_rows(): return lax.all_to_all(tiled, axis, 0, 0, tiled=True)  11.6 us
  transfers between devices with their start and end apart: 2, of which 2 were waited for; matrix products, arithmetic and copies ran while one was open for 3% of the time, Pallas kernels for 0%

profile of v1, /device:TPU:8, one launch (start us, length us, event | category | flops | bytes accessed | tf_op | source)
XLA Modules:
  0.0 458.4 jit_solution(11790363953714760026)
XLA Ops:
  0.6 0.9 pad_maximum_fusion.5
  1.5 2.5 tile.4
  4.0 11.6 %all-to-all-start = ((bf16[32,32,2048]{2,1,0:T(8,128)(2,1)}), bf16[32,32,2048]{2,1,0:T(8,128)(2,1)}, u32[]{:S(2)}, u32[]{:S(2)}) async-start(bf16[32,32,2048]{2,1,0:T(8,128)(2,1)} %tile.4), calls=%async_computation | async-start | bytes 8388608 | tf_op jit(solution)/shard_map/all_to_all | solution.py:22
  15.9 0.3 mul.87
  16.2 0.3 mul.90
  16.6 1.3 bitcast_multiply_fusion.4
  17.9 92.1 %all-to-all-done = bf16[32,32,2048]{2,1,0:T(8,128)(2,1)} async-done(((bf16[32,32,2048]{2,1,0:T(8,128)(2,1)}), bf16[32,32,2048]{2,1,0:T(8,128)(2,1)}, u32[]{:S(2)}, u32[]{:S(2)}) %all-to-all-start) | async-done | bytes 4194336 | tf_op jit(solution)/shard_map/all_to_all | solution.py:22
  109.9 4.4 fusion.9
  114.3 0.2 mul.93
  114.6 1.0 copy-done
  115.5 2.9 fusion.6
  118.4 0.4 copy_bitcast_fusion
  118.8 76.3 %all_to_all.36 = f32[8,128,1536]{1,2,0:T(8,128)} all-to-all(f32[8,128,1536]{1,2,0:T(8,128)S(1)} %copy_bitcast_fusion), channel_id=1, replica_groups=mesh['row'=32,'col'=8] {'col'}, dimensions={0} | all-to-all | bytes 12582912 | tf_op jit(solution)/shard_map/all_to_all | solution.py:26
  195.1 3.2 reduce_sum.18
  198.3 0.2 multiply_convert_fusion.2
  198.5 0.2 copy.26
  198.7 0.3 tile.5
  199.0 40.6 %all_to_all.37 = bf16[8,128,1536]{2,1,0:T(8,128)(2,1)S(1)} all-to-all(bf16[8,128,1536]{2,1,0:T(8,128)(2,1)S(1)} %tile.5), channel_id=1, replica_groups=mesh['row'=32,'col'=8] {'col'}, dimensions={0} | all-to-all | bytes 6291456 | tf_op jit(solution)/shard_map/all_to_all | solution.py:22
  239.6 2.4 fusion.2
  242.0 1.3 fusion.14
  243.3 4.1 pad_maximum_fusion
  247.4 9.2 %copy.27 = f32[1024,2048]{1,0:T(8,128)} copy(f32[1024,2048]{0,1:T(8,128)} %pad_maximum_fusion) | data formatting | bytes 16777216 | tf_op jit(solution)/shard_map/concatenate | solution.py:66
  256.6 7.2 %all-to-all-start.3 = ((f32[32,32,2048]{2,1,0:T(8,128)}), f32[32,32,2048]{2,1,0:T(8,128)}, u32[]{:S(2)}, u32[]{:S(2)}) async-start(f32[32,32,2048]{2,1,0:T(8,128)} %bitcast.34), calls=%async_computation.3 | async-start | bytes 16777216 | tf_op jit(solution)/shard_map/all_to_all | solution.py:26
  264.0 0.2 mul.109
  264.2 4.3 bitcast_multiply_fusion
  268.5 4.0 fusion
  272.5 0.3 mul.103
  272.8 0.3 mul.106
  273.2 3.0 bitcast_multiply_fusion.1
  276.2 177.7 %all-to-all-done.3 = f32[32,32,2048]{2,1,0:T(8,128)} async-done(((f32[32,32,2048]{2,1,0:T(8,128)}), f32[32,32,2048]{2,1,0:T(8,128)}, u32[]{:S(2)}, u32[]{:S(2)}) %all-to-all-start.3) | async-done | bytes 8388640 | tf_op jit(solution)/shard_map/all_to_all | solution.py:26
  453.9 3.8 reduce_sum.19
  457.7 0.7 fusion.19
  (31 shorter events, 0.4 us)
Async XLA Ops:
  4.0 11.6 %copy-start.9 = (s32[8,4]{0,1:T(4,128)S(1)}, s32[8,4]{0,1:T(4,128)}, u32[]{:S(2)}) copy-start(s32[8,4]{0,1:T(4,128)} %param.13) | copy-start | bytes 388
  4.0 11.7 %copy-start.10 = (s32[8,4]{0,1:T(4,128)S(1)}, s32[8,4]{0,1:T(4,128)}, u32[]{:S(2)}) copy-start(s32[8,4]{0,1:T(4,128)} %param.14) | copy-start | bytes 388
  4.0 11.8 %copy-start.11 = (s32[4,8]{1,0:T(4,128)S(1)}, s32[4,8]{1,0:T(4,128)}, u32[]{:S(2)}) copy-start(s32[4,8]{1,0:T(4,128)} %param.15) | copy-start | bytes 388
  4.0 12.5 %copy-start.4 = (bf16[1024,512]{1,0:T(8,128)(2,1)S(1)}, bf16[1024,512]{1,0:T(8,128)(2,1)}, u32[]{:S(2)}) copy-start(bf16[1024,512]{1,0:T(8,128)(2,1)} %param.11) | copy-start | bytes 3145732
  4.0 12.5 %copy-start.5 = (bf16[1024,512]{1,0:T(8,128)(2,1)S(1)}, bf16[1024,512]{1,0:T(8,128)(2,1)}, u32[]{:S(2)}) copy-start(bf16[1024,512]{1,0:T(8,128)(2,1)} %param.10) | copy-start | bytes 3145732
  4.0 105.9 %all-to-all-start = ((bf16[32,32,2048]{2,1,0:T(8,128)(2,1)}), bf16[32,32,2048]{2,1,0:T(8,128)(2,1)}, u32[]{:S(2)}, u32[]{:S(2)}) async-start(bf16[32,32,2048]{2,1,0:T(8,128)(2,1)} %tile.4), calls=%async_computation | async-start | bytes 8388608 | tf_op jit(solution)/shard_map/all_to_all | solution.py:22
  17.9 96.5 %copy-start.6 = (bf16[1024,512]{1,0:T(8,128)(2,1)}, bf16[1024,512]{1,0:T(8,128)(2,1)S(1)}, u32[]{:S(2)}) copy-start(bf16[1024,512]{1,0:T(8,128)(2,1)S(1)} %get-tuple-element.18) | copy-start | bytes 3145732
  109.9 5.6 %copy-start.2 = (bf16[512,1024]{1,0:T(8,128)(2,1)S(1)}, bf16[512,1024]{1,0:T(8,128)(2,1)}, u32[]{:S(2)}) copy-start(bf16[512,1024]{1,0:T(8,128)(2,1)} %param.12) | copy-start | bytes 3145732
  114.5 1.0 copy-start
  199.0 40.6 %copy-start.7 = (bf16[1024,512]{1,0:T(8,128)(2,1)S(1)}, bf16[1024,512]{1,0:T(8,128)(2,1)}, u32[]{:S(2)}) copy-start(bf16[1024,512]{1,0:T(8,128)(2,1)} %copy-done.6) | copy-start | bytes 3145732
  199.0 40.6 %copy-start.8 = (bf16[1024,512]{1,0:T(8,128)(2,1)S(1)}, bf16[1024,512]{1,0:T(8,128)(2,1)}, u32[]{:S(2)}) copy-start(bf16[1024,512]{1,0:T(8,128)(2,1)} %get-tuple-element.19) | copy-start | bytes 3145732
  239.6 2.4 copy-start.1
  239.6 2.4 copy-start.3
  256.6 197.2 %all-to-all-start.3 = ((f32[32,32,2048]{2,1,0:T(8,128)}), f32[32,32,2048]{2,1,0:T(8,128)}, u32[]{:S(2)}, u32[]{:S(2)}) async-start(f32[32,32,2048]{2,1,0:T(8,128)} %bitcast.34), calls=%async_computation.3 | async-start | bytes 16777216 | tf_op jit(solution)/shard_map/all_to_all | solution.py:26

commit v2 on v1

--- a/solution.py
+++ b/solution.py
@@ -1,9 +1,13 @@
 import jax
 import jax.numpy as jnp
+import numpy as np
 from jax import lax
+from jax.sharding import Mesh
 from jax.sharding import PartitionSpec as P
 
 BLOCK = 128
+ROW = ("z", "x")
+COL = ("y", "core")
 
 
 contract_inner = (((1,), (1,)), ((), ()))
@@ -22,18 +26,39 @@
     return lax.all_to_all(tiled, axis, 0, 0, tiled=True)
 
 
-def reduce_rows(x, axis, n):
-    got = lax.all_to_all(x, axis, 0, 0, tiled=True)
-    rows = x.shape[0] // n
-    return jnp.sum(got.reshape(n, rows, x.shape[1]), axis=0)
+def ring_rs(x, axis, n, d):
+    c = x.shape[0] // n
+    i = lax.axis_index(axis)
+    chunks = x.reshape((n, c) + x.shape[1:])
+    perm = [(j, (j + d) % n) for j in range(n)]
+    acc = lax.dynamic_index_in_dim(chunks, (i - d) % n, 0, keepdims=False)
+    for s in range(1, n):
+        own = lax.dynamic_index_in_dim(chunks, (i - d * (s + 1)) % n, 0, keepdims=False)
+        acc = lax.ppermute(acc, axis, perm) + own
+    return acc
 
 
-def shards(tokens, cotangent, gate_weight, up_weight, down_weight, gate_mask, up_mask, down_mask):
-    n_row = lax.axis_size("row")
-    n_col = lax.axis_size("col")
+def row_reduce(x, nz, nx):
+    rows, w = x.shape
+    c = rows // (nz * nx)
+    q = w // 4
+    outs = []
+    for j in range(4):
+        p = x[:, j * q:(j + 1) * q]
+        d = 1 if j % 2 == 0 else -1
+        if j < 2:
+            outs.append(ring_rs(ring_rs(p, "z", nz, d), "x", nx, d))
+        else:
+            p = p.reshape(nz, nx, c, q).transpose(1, 0, 2, 3).reshape(rows, q)
+            outs.append(ring_rs(ring_rs(p, "x", nx, d), "z", nz, d))
+    return jnp.concatenate(outs, axis=1)
+
+
+def shards(nz, nx, ny, nc, tokens, cotangent, gate_weight, up_weight, down_weight, gate_mask, up_mask, down_mask):
     hidden_width = gate_weight.shape[1]
     features = tokens.shape[1]
-    both = gather_rows(jnp.concatenate([tokens, cotangent], axis=1), "row", n_row)
+    local = jnp.concatenate([tokens, cotangent], axis=1)
+    both = lax.all_gather(lax.all_gather(local, "x", axis=0, tiled=True), "z", axis=0, tiled=True)
     gathered_tokens = both[:, :features]
     gathered_grads = both[:, features:]
     joint_weight = jnp.concatenate(
@@ -44,7 +69,9 @@
     hidden_part = lax.dot_general(
         gathered_grads, masked_down, contract_inner, preferred_element_type=jnp.float32
     )
-    sums = reduce_rows(jnp.concatenate([joint_part, hidden_part], axis=1), "col", n_col)
+    sums = lax.psum_scatter(
+        jnp.concatenate([joint_part, hidden_part], axis=1), COL, scatter_dimension=0, tiled=True
+    )
     gate_pre = sums[:, :hidden_width]
     up_pre = sums[:, hidden_width:2 * hidden_width]
     grad_hidden = sums[:, 2 * hidden_width:]
@@ -56,14 +83,14 @@
     rows = jnp.concatenate(
         [hidden_rows, grad_gate_pre.astype(jnp.bfloat16), grad_up_pre.astype(jnp.bfloat16)], axis=1
     )
-    full = gather_rows(rows, "col", n_col)
+    full = gather_rows(rows, COL, ny * nc)
     hidden = full[:, :hidden_width]
     joint_grad = full[:, hidden_width:]
     output_term = jnp.dot(hidden, masked_down, preferred_element_type=jnp.float32)
     token_term = lax.dot_general(
         joint_grad, joint_weight, contract_inner, preferred_element_type=jnp.float32
     )
-    outs = reduce_rows(jnp.concatenate([output_term, token_term], axis=1), "row", n_row)
+    outs = row_reduce(jnp.concatenate([output_term, token_term], axis=1), nz, nx)
     layer_out = outs[:, :features]
     grad_tokens = outs[:, features:]
     weight_grads = lax.dot_general(
@@ -84,22 +111,23 @@
     )
 
 
+def physical_split(devices, coord):
+    coords = [getattr(d, "coords", None) for d in devices]
+    if any(c is None for c in coords):
+        return None
+    return len({c[coord] for c in coords})
+
+
 def solution(mesh):
-    in_specs = (
-        P("row", "col"),
-        P("row", "col"),
-        P("col", "row"),
-        P("col", "row"),
-        P("row", "col"),
-        P("col", "row"),
-        P("col", "row"),
-        P("row", "col"),
-    )
-    out_specs = (
-        P("row", "col"),
-        P("row", "col"),
-        P("col", "row"),
-        P("col", "row"),
-        P("row", "col"),
-    )
-    return jax.shard_map(shards, mesh=mesh, in_specs=in_specs, out_specs=out_specs, check_vma=False)
+    n_row, n_col = mesh.shape["row"], mesh.shape["col"]
+    devs = mesh.devices
+    nx = physical_split(list(devs[:, 0]), 0) or 4
+    nz = n_row // nx
+    nc = 2
+    ny = n_col // nc
+    m4 = Mesh(np.asarray(devs).reshape(nz, nx, ny, nc), ("z", "x", "y", "core"))
+    a, w = P(ROW, COL), P(COL, ROW)
+    in_specs = (a, a, w, w, a, w, w, a)
+    out_specs = (a, a, w, w, a)
+    body = lambda *args: shards(nz, nx, ny, nc, *args)
+    return jax.shard_map(body, mesh=m4, in_specs=in_specs, out_specs=out_specs, check_vma=False)

time: 462 us -> 311 us (0.67)
  waiting for transfers between devices: 270 us -> 156 us
  blocking collectives: 117 us -> 13.9 us
  starting transfers between devices: 18.8 us -> 82.3 us
  between operations: 0.88 us -> 14.9 us
  local copies, waits for them, and re-layouts: 15.9 us -> 6.68 us
    all_to_all x1 -> x0, waiting for transfers between devices: 178 us -> none  [reduce_rows(): got = lax.all_to_all(x, axis, 0, 0, tiled=True)]
    all_to_all x2 -> x0, blocking collectives: 117 us -> none  [the longest x1 76.3 us: reduce_rows(): got = lax.all_to_all(x, axis, 0, 0, tiled=True)]
    ppermute x0 -> x40, starting transfers between devices: none -> 76.2 us  [ring_rs(): acc = lax.ppermute(acc, axis, perm) + own]
    all_to_all x1, waiting for transfers between devices: 92.1 us -> 36.8 us  [gather_rows(): return lax.all_to_all(tiled, axis, 0, 0, tiled=True)]
    all_gather x0 -> x1, waiting for transfers between devices: none -> 53 us  [shards(): lax.all_gather(lax.all_gather(local, 'x', axis=0, tiled=True), 'z', axis=...]
    reduce_scatter x0 -> x1, waiting for transfers between devices: none -> 41.8 us  [shards(): lax.psum_scatter(jnp.concatenate([joint_part, hidden_part], axis=1), COL,...]
    ppermute x0 -> x40, waiting for transfers between devices: none -> 24.1 us  [ring_rs(): acc = lax.ppermute(acc, axis, perm) + own]
    all_gather x0 -> x1, blocking collectives: none -> 13.9 us  [shards(): lax.all_gather(local, 'x', axis=0, tiled=True)]
  transfers between devices with their start and end apart: 2 -> 43, of which waited for: 2 -> 15; matrix products, arithmetic and copies ran while one was open for 3% -> 5% of each run, Pallas kernels for 0% -> 0%
where the time goes in v2:
time: 311 us; the launch traced here: 305 us
  waiting for transfers between devices  156 us (50%)
  starting transfers between devices  82.3 us (26%)
  matrix products  16.5 us (5%)
  other arithmetic  15.2 us (5%)
  between operations  14.9 us (5%)
  blocking collectives  13.9 us (4%)
  local copies, waits for them, and re-layouts  6.68 us (2%)
    ppermute x40, starting transfers between devices, ring_rs(): acc = lax.ppermute(acc, axis, perm) + own  76.2 us
    all_gather x1, waiting for transfers between devices, shards(): lax.all_gather(lax.all_gather(local, 'x', axis=0, tiled=True), 'z', axis=...  53 us
    reduce_scatter x1, waiting for transfers between devices, shards(): lax.psum_scatter(jnp.concatenate([joint_part, hidden_part], axis=1), COL,...  41.8 us
    all_to_all x1, waiting for transfers between devices, gather_rows(): return lax.all_to_all(tiled, axis, 0, 0, tiled=True)  36.8 us
    ppermute x40, waiting for transfers between devices, ring_rs(): acc = lax.ppermute(acc, axis, perm) + own  24.1 us
    all_gather x1, blocking collectives, shards(): lax.all_gather(local, 'x', axis=0, tiled=True)  13.9 us
  transfers between devices with their start and end apart: 43, of which 15 were waited for; matrix products, arithmetic and copies ran while one was open for 5% of the time, Pallas kernels for 0%

profile of v2, /device:TPU:8, one launch (start us, length us, event | category | flops | bytes accessed | tf_op | source)
XLA Modules:
  0.0 305.3 jit_solution(2127318133923769499)
XLA Ops:
  8.3 13.9 %all_gather.6 = bf16[128,2048]{1,0:T(8,128)(2,1)} all-gather(bf16[32,2048]{1,0:T(8,128)(2,1)S(1)} %pad_maximum_fusion.5), channel_id=1, replica_groups=mesh['z'=8,'x'=4,'y'=4,'core'=2] {'x'}, dimensions={0}, use_global_device_ids=true | all-gather | bytes 655360 | tf_op jit(solution)/shard_map/all_gather | solution.py:61
  27.0 53.0 %all-gather.2.cloned.1.call-done = bf16[1024,2048]{1,0:T(8,128)(2,1)} async-done(((bf16[128,2048]{1,0:T(8,128)(2,1)}), bf16[1024,2048]{1,0:T(8,128)(2,1)}) %all-gather.2.cloned.1.call-update) | async-done | bytes 4194320 | tf_op jit(solution)/shard_map/all_gather | solution.py:61
  80.1 4.8 %fusion.9 = f32[1024,1024]{0,1:T(8,128)S(1)} fusion(bf16[1024,2048]{1,0:T(8,128)(2,1)} %all-gather.2.cloned.1.call-done, bf16[1024,512]{1,0:T(8,128)(2,1)} %get-tuple-element.20, bf16[1024,512]{1,0:T(8,128)(2,1)} %get-tuple-element.21), kind=kOutput, calls=%fused_computation.14 | convolution fusion | flops 2151677952 | bytes 8388608 | tf_op jit(solution)/shard_map/dot_general | solution.py:68
  87.4 3.2 %pad_maximum_fusion = f32[1024,1536]{0,1:T(8,128)} fusion(f32[1024,512]{0,1:T(8,128)S(1)} %fusion.6, f32[1024,1024]{0,1:T(8,128)S(1)} %fusion.9), kind=kLoop, calls=%fused_computation | loop fusion | flops 1572864 | bytes 12582912 | tf_op jit(solution)/shard_map/concatenate | solution.py:73
  90.6 41.8 %reduce-scatter.2.cloned.1.call-done = f32[128,1536]{0,1:T(8,128)} async-done(((f32[1024,1536]{0,1:T(8,128)}), f32[128,1536]{0,1:T(8,128)}) %reduce-scatter.2.cloned.1.call-update) | async-done | bytes 786448 | tf_op jit(solution)/shard_map/reduce_scatter | solution.py:72
  135.8 6.1 %all-to-all-start = ((bf16[8,128,1536]{2,1,0:T(8,128)(2,1)}), bf16[8,128,1536]{2,1,0:T(8,128)(2,1)S(1)}, u32[]{:S(2)}, u32[]{:S(2)}) async-start(bf16[8,128,1536]{2,1,0:T(8,128)(2,1)} %tile.2), calls=%async_computation.1 | async-start | bytes 6291456 | tf_op jit(solution)/shard_map/all_to_all | solution.py:26
  142.1 36.8 %all-to-all-done = bf16[8,128,1536]{2,1,0:T(8,128)(2,1)S(1)} async-done(((bf16[8,128,1536]{2,1,0:T(8,128)(2,1)}), bf16[8,128,1536]{2,1,0:T(8,128)(2,1)S(1)}, u32[]{:S(2)}, u32[]{:S(2)}) %all-to-all-start) | async-done | bytes 3145760 | tf_op jit(solution)/shard_map/all_to_all | solution.py:26
  178.9 4.1 %fusion.2 = f32[1024,1024]{1,0:T(8,128)S(1)} fusion(bf16[1024,1536]{1,0:T(8,128)(2,1)S(1)} %bitcast.173, bf16[1024,512]{1,0:T(8,128)(2,1)} %get-tuple-element.20, bf16[1024,512]{1,0:T(8,128)(2,1)} %get-tuple-element.21), kind=kOutput, calls=%fused_computation.7 | convolution fusion | flops 2151677952 | bytes 8388608 | tf_op jit(solution)/shard_map/dot_general | solution.py:90
  192.9 2.4 fusion
  196.1 3.0 bitcast_multiply_fusion.1
  199.3 2.7 bitcast_multiply_fusion
  202.4 3.1 %collective-permute-start.11 = (f32[128,512]{1,0:T(8,128)S(1)}, f32[128,512]{1,0:T(8,128)S(1)}, u32[]{:S(2)}, u32[]{:S(2)}) collective-permute-start(f32[128,512]{1,0:T(8,128)S(1)} %bitcast_add_fusion.12), channel_id=1, source_target_pairs={{0,224},{32,0},{64,32},{96,64},{128,96},{160,128},{192,160},{224,1... | collective-permute-start | bytes 786440 | tf_op jit(solution)/shard_map/ppermute | solution.py:37
  205.9 4.3 %collective-permute-done.1 = f32[128,512]{1,0:T(8,128)S(1)} collective-permute-done((f32[128,512]{1,0:T(8,128)S(1)}, f32[128,512]{1,0:T(8,128)S(1)}, u32[]{:S(2)}, u32[]{:S(2)}) %collective-permute-start.1) | collective-permute-done | bytes 262176 | tf_op jit(solution)/shard_map/ppermute | solution.py:37
  210.4 3.3 %collective-permute-start.12 = (f32[128,512]{1,0:T(8,128)S(1)}, f32[128,512]{1,0:T(8,128)S(1)}, u32[]{:S(2)}, u32[]{:S(2)}) collective-permute-start(f32[128,512]{1,0:T(8,128)S(1)} %bitcast_add_fusion.11), channel_id=1, source_target_pairs={{0,224},{32,0},{64,32},{96,64},{128,96},{160,128},{192,160},{224,1... | collective-permute-start | bytes 786440 | tf_op jit(solution)/shard_map/ppermute | solution.py:37
  215.4 2.6 collective-permute-done.2
  218.0 9.0 %collective-permute-start.3 = (f32[128,512]{1,0:T(8,128)S(1)}, f32[128,512]{1,0:T(8,128)S(1)}, u32[]{:S(2)}, u32[]{:S(2)}) collective-permute-start(f32[128,512]{1,0:T(8,128)S(1)} %bitcast_add_fusion.17), channel_id=1, source_target_pairs={{0,32},{32,64},{64,96},{96,128},{128,160},{160,192},{192,224},{224... | collective-permute-start | bytes 786440 | tf_op jit(solution)/shard_map/ppermute | solution.py:37
  227.0 3.3 %collective-permute-start.13 = (f32[128,512]{1,0:T(8,128)S(1)}, f32[128,512]{1,0:T(8,128)S(1)}, u32[]{:S(2)}, u32[]{:S(2)}) collective-permute-start(f32[128,512]{1,0:T(8,128)S(1)} %bitcast_add_fusion.10), channel_id=1, source_target_pairs={{0,224},{32,0},{64,32},{96,64},{128,96},{160,128},{192,160},{224,1... | collective-permute-start | bytes 786440 | tf_op jit(solution)/shard_map/ppermute | solution.py:37
  230.8 4.0 %collective-permute-done.3 = f32[128,512]{1,0:T(8,128)S(1)} collective-permute-done((f32[128,512]{1,0:T(8,128)S(1)}, f32[128,512]{1,0:T(8,128)S(1)}, u32[]{:S(2)}, u32[]{:S(2)}) %collective-permute-start.3) | collective-permute-done | bytes 262176 | tf_op jit(solution)/shard_map/ppermute | solution.py:37
  234.9 3.6 %collective-permute-start.14 = (f32[128,512]{1,0:T(8,128)S(1)}, f32[128,512]{1,0:T(8,128)S(1)}, u32[]{:S(2)}, u32[]{:S(2)}) collective-permute-start(f32[128,512]{1,0:T(8,128)S(1)} %bitcast_add_fusion.9), channel_id=1, source_target_pairs={{0,224},{32,0},{64,32},{96,64},{128,96},{160,128},{192,160},{224,1... | collective-permute-start | bytes 786440 | tf_op jit(solution)/shard_map/ppermute | solution.py:37
  240.5 3.0 collective-permute-done.4
  243.8 3.8 %collective-permute-start.15 = (f32[128,512]{1,0:T(8,128)S(1)}, f32[128,512]{1,0:T(8,128)S(1)}, u32[]{:S(2)}, u32[]{:S(2)}) collective-permute-start(f32[128,512]{1,0:T(8,128)S(1)} %bitcast_add_fusion.8), channel_id=1, source_target_pairs={{0,224},{32,0},{64,32},{96,64},{128,96},{160,128},{192,160},{224,1... | collective-permute-start | bytes 786440 | tf_op jit(solution)/shard_map/ppermute | solution.py:37
  248.0 3.2 %collective-permute-start.33 = (f32[32,512]{1,0:T(8,128)S(1)}, f32[32,512]{1,0:T(8,128)S(1)}, u32[]{:S(2)}, u32[]{:S(2)}) collective-permute-start(f32[32,512]{1,0:T(8,128)S(1)} %dynamic-slice_bitcast_fusion.4), channel_id=1, source_target_pairs={{0,224},{32,0},{64,32},{96,64},{128,96},{160,128},{192,160},{224,1... | collective-permute-start | bytes 196616 | tf_op jit(solution)/shard_map/ppermute | solution.py:37
  251.2 2.2 collective-permute-done.5
  254.0 3.8 %collective-permute-start.16 = (f32[128,512]{1,0:T(8,128)S(1)}, f32[128,512]{1,0:T(8,128)S(1)}, u32[]{:S(2)}, u32[]{:S(2)}) collective-permute-start(f32[128,512]{1,0:T(8,128)S(1)} %bitcast_add_fusion.7), channel_id=1, source_target_pairs={{0,224},{32,0},{64,32},{96,64},{128,96},{160,128},{192,160},{224,1... | collective-permute-start | bytes 786440 | tf_op jit(solution)/shard_map/ppermute | solution.py:37
  257.9 3.3 %collective-permute-start.34 = (f32[32,512]{1,0:T(8,128)S(1)}, f32[32,512]{1,0:T(8,128)S(1)}, u32[]{:S(2)}, u32[]{:S(2)}) collective-permute-start(f32[32,512]{1,0:T(8,128)S(1)} %bitcast_add_fusion.26), channel_id=1, source_target_pairs={{0,224},{32,0},{64,32},{96,64},{128,96},{160,128},{192,160},{224,1... | collective-permute-start | bytes 196616 | tf_op jit(solution)/shard_map/ppermute | solution.py:37
  263.5 3.6 %collective-permute-start.35 = (f32[32,512]{1,0:T(8,128)S(1)}, f32[32,512]{1,0:T(8,128)S(1)}, u32[]{:S(2)}, u32[]{:S(2)}) collective-permute-start(f32[32,512]{1,0:T(8,128)S(1)} %bitcast_add_fusion.25), channel_id=1, source_target_pairs={{0,224},{32,0},{64,32},{96,64},{128,96},{160,128},{192,160},{224,1... | collective-permute-start | bytes 196616 | tf_op jit(solution)/shard_map/ppermute | solution.py:37
  269.0 3.6 %collective-permute-start.36 = (f32[32,512]{1,0:T(8,128)S(1)}, f32[32,512]{1,0:T(8,128)S(1)}, u32[]{:S(2)}, u32[]{:S(2)}) collective-permute-start(f32[32,512]{1,0:T(8,128)S(1)} %bitcast_add_fusion.24), channel_id=1, source_target_pairs={{0,224},{32,0},{64,32},{96,64},{128,96},{160,128},{192,160},{224,1... | collective-permute-start | bytes 196616 | tf_op jit(solution)/shard_map/ppermute | solution.py:37
  274.6 3.6 %collective-permute-start.37 = (f32[32,512]{1,0:T(8,128)S(1)}, f32[32,512]{1,0:T(8,128)S(1)}, u32[]{:S(2)}, u32[]{:S(2)}) collective-permute-start(f32[32,512]{1,0:T(8,128)S(1)} %bitcast_add_fusion.23), channel_id=1, source_target_pairs={{0,224},{32,0},{64,32},{96,64},{128,96},{160,128},{192,160},{224,1... | collective-permute-start | bytes 196616 | tf_op jit(solution)/shard_map/ppermute | solution.py:37
  281.8 3.3 %collective-permute-start.38 = (f32[32,512]{1,0:T(8,128)S(1)}, f32[32,512]{1,0:T(8,128)S(1)}, u32[]{:S(2)}, u32[]{:S(2)}) collective-permute-start(f32[32,512]{1,0:T(8,128)S(1)} %bitcast_add_fusion.22), channel_id=1, source_target_pairs={{0,224},{32,0},{64,32},{96,64},{128,96},{160,128},{192,160},{224,1... | collective-permute-start | bytes 196616 | tf_op jit(solution)/shard_map/ppermute | solution.py:37
  286.0 2.6 collective-permute-start.18
  288.7 3.3 %collective-permute-start.39 = (f32[32,512]{1,0:T(8,128)S(1)}, f32[32,512]{1,0:T(8,128)S(1)}, u32[]{:S(2)}, u32[]{:S(2)}) collective-permute-start(f32[32,512]{1,0:T(8,128)S(1)} %bitcast_add_fusion.21), channel_id=1, source_target_pairs={{0,224},{32,0},{64,32},{96,64},{128,96},{160,128},{192,160},{224,1... | collective-permute-start | bytes 196616 | tf_op jit(solution)/shard_map/ppermute | solution.py:37
  292.1 3.3 %collective-permute-start.19 = (f32[32,512]{1,0:T(8,128)S(1)}, f32[32,512]{1,0:T(8,128)S(1)}, u32[]{:S(2)}, u32[]{:S(2)}) collective-permute-start(f32[32,512]{1,0:T(8,128)S(1)} %bitcast_add_fusion.35), channel_id=1, source_target_pairs={{0,24},{8,0},{16,8},{24,16},{1,25},{9,1},{17,9},{25,17},{2,26},{10... | collective-permute-start | bytes 196616 | tf_op jit(solution)/shard_map/ppermute | solution.py:37
  (154 shorter events, 43.0 us)
Async XLA Ops:
  7.2 72.9 %all-gather.2.cloned.1.call-start = ((), (), s32[]{:S(2)}) async-start(), calls=%async_computation.2 | async-start | bytes 4718592 | tf_op jit(solution)/shard_map/all_gather | solution.py:61
  22.2 110.3 %reduce-scatter.2.cloned.1.call-start = ((), (), s32[]{:S(2)}) async-start(), calls=%async_computation.3 | async-start | bytes 7077888 | tf_op jit(solution)/shard_map/reduce_scatter | solution.py:72
  135.8 43.1 %all-to-all-start = ((bf16[8,128,1536]{2,1,0:T(8,128)(2,1)}), bf16[8,128,1536]{2,1,0:T(8,128)(2,1)S(1)}, u32[]{:S(2)}, u32[]{:S(2)}) async-start(bf16[8,128,1536]{2,1,0:T(8,128)(2,1)} %tile.2), calls=%async_computation.1 | async-start | bytes 6291456 | tf_op jit(solution)/shard_map/all_to_all | solution.py:26
  185.0 20.4 %collective-permute-start.20 = (f32[256,512]{1,0:T(8,128)S(1)}, f32[256,512]{1,0:T(8,128)S(1)}, u32[]{:S(2)}, u32[]{:S(2)}) collective-permute-start(f32[256,512]{1,0:T(8,128)S(1)} %dynamic-slice_bitcast_fusion.1), channel_id=1, source_target_pairs={{0,8},{8,16},{16,24},{24,0},{1,9},{9,17},{17,25},{25,1},{2,10},{10... | collective-permute-start | bytes 1572872 | tf_op jit(solution)/shard_map/ppermute | solution.py:37
  186.8 26.9 %collective-permute-start.30 = (f32[256,512]{1,0:T(8,128)S(1)}, f32[256,512]{1,0:T(8,128)S(1)}, u32[]{:S(2)}, u32[]{:S(2)}) collective-permute-start(f32[256,512]{1,0:T(8,128)S(1)} %dynamic-slice_bitcast_fusion), channel_id=1, source_target_pairs={{0,24},{8,0},{16,8},{24,16},{1,25},{9,1},{17,9},{25,17},{2,26},{10... | collective-permute-start | bytes 1572872 | tf_op jit(solution)/shard_map/ppermute | solution.py:37
  189.4 12.6 %collective-permute-start = (f32[128,512]{1,0:T(8,128)S(1)}, f32[128,512]{1,0:T(8,128)S(1)}, u32[]{:S(2)}, u32[]{:S(2)}) collective-permute-start(f32[128,512]{1,0:T(8,128)S(1)} %dynamic-slice_bitcast_fusion.3), channel_id=1, source_target_pairs={{0,32},{32,64},{64,96},{96,128},{128,160},{160,192},{192,224},{224... | collective-permute-start | bytes 786440 | tf_op jit(solution)/shard_map/ppermute | solution.py:37
  191.1 11.3 %collective-permute-start.10 = (f32[128,512]{1,0:T(8,128)S(1)}, f32[128,512]{1,0:T(8,128)S(1)}, u32[]{:S(2)}, u32[]{:S(2)}) collective-permute-start(f32[128,512]{1,0:T(8,128)S(1)} %dynamic-slice_bitcast_fusion.2), channel_id=1, source_target_pairs={{0,224},{32,0},{64,32},{96,64},{128,96},{160,128},{192,160},{224,1... | collective-permute-start | bytes 786440 | tf_op jit(solution)/shard_map/ppermute | solution.py:37
  202.0 8.2 %collective-permute-start.1 = (f32[128,512]{1,0:T(8,128)S(1)}, f32[128,512]{1,0:T(8,128)S(1)}, u32[]{:S(2)}, u32[]{:S(2)}) collective-permute-start(f32[128,512]{1,0:T(8,128)S(1)} %bitcast_add_fusion.19), channel_id=1, source_target_pairs={{0,32},{32,64},{64,96},{96,128},{128,160},{160,192},{192,224},{224... | collective-permute-start | bytes 786440 | tf_op jit(solution)/shard_map/ppermute | solution.py:37
  202.4 8.0 %collective-permute-start.11 = (f32[128,512]{1,0:T(8,128)S(1)}, f32[128,512]{1,0:T(8,128)S(1)}, u32[]{:S(2)}, u32[]{:S(2)}) collective-permute-start(f32[128,512]{1,0:T(8,128)S(1)} %bitcast_add_fusion.12), channel_id=1, source_target_pairs={{0,224},{32,0},{64,32},{96,64},{128,96},{160,128},{192,160},{224,1... | collective-permute-start | bytes 786440 | tf_op jit(solution)/shard_map/ppermute | solution.py:37
  205.5 24.7 %collective-permute-start.21 = (f32[256,512]{1,0:T(8,128)S(1)}, f32[256,512]{1,0:T(8,128)S(1)}, u32[]{:S(2)}, u32[]{:S(2)}) collective-permute-start(f32[256,512]{1,0:T(8,128)S(1)} %bitcast_add_fusion.5), channel_id=1, source_target_pairs={{0,8},{8,16},{16,24},{24,0},{1,9},{9,17},{17,25},{25,1},{2,10},{10... | collective-permute-start | bytes 1572872 | tf_op jit(solution)/shard_map/ppermute | solution.py:37
  210.3 7.7 %collective-permute-start.2 = (f32[128,512]{1,0:T(8,128)S(1)}, f32[128,512]{1,0:T(8,128)S(1)}, u32[]{:S(2)}, u32[]{:S(2)}) collective-permute-start(f32[128,512]{1,0:T(8,128)S(1)} %bitcast_add_fusion.18), channel_id=1, source_target_pairs={{0,32},{32,64},{64,96},{96,128},{128,160},{160,192},{192,224},{224... | collective-permute-start | bytes 786440 | tf_op jit(solution)/shard_map/ppermute | solution.py:37
  210.4 16.5 %collective-permute-start.12 = (f32[128,512]{1,0:T(8,128)S(1)}, f32[128,512]{1,0:T(8,128)S(1)}, u32[]{:S(2)}, u32[]{:S(2)}) collective-permute-start(f32[128,512]{1,0:T(8,128)S(1)} %bitcast_add_fusion.11), channel_id=1, source_target_pairs={{0,224},{32,0},{64,32},{96,64},{128,96},{160,128},{192,160},{224,1... | collective-permute-start | bytes 786440 | tf_op jit(solution)/shard_map/ppermute | solution.py:37
  213.8 24.7 %collective-permute-start.31 = (f32[256,512]{1,0:T(8,128)S(1)}, f32[256,512]{1,0:T(8,128)S(1)}, u32[]{:S(2)}, u32[]{:S(2)}) collective-permute-start(f32[256,512]{1,0:T(8,128)S(1)} %bitcast_add_fusion.2), channel_id=1, source_target_pairs={{0,24},{8,0},{16,8},{24,16},{1,25},{9,1},{17,9},{25,17},{2,26},{10... | collective-permute-start | bytes 1572872 | tf_op jit(solution)/shard_map/ppermute | solution.py:37
  218.0 16.8 %collective-permute-start.3 = (f32[128,512]{1,0:T(8,128)S(1)}, f32[128,512]{1,0:T(8,128)S(1)}, u32[]{:S(2)}, u32[]{:S(2)}) collective-permute-start(f32[128,512]{1,0:T(8,128)S(1)} %bitcast_add_fusion.17), channel_id=1, source_target_pairs={{0,32},{32,64},{64,96},{96,128},{128,160},{160,192},{192,224},{224... | collective-permute-start | bytes 786440 | tf_op jit(solution)/shard_map/ppermute | solution.py:37
  227.0 7.9 %collective-permute-start.13 = (f32[128,512]{1,0:T(8,128)S(1)}, f32[128,512]{1,0:T(8,128)S(1)}, u32[]{:S(2)}, u32[]{:S(2)}) collective-permute-start(f32[128,512]{1,0:T(8,128)S(1)} %bitcast_add_fusion.10), channel_id=1, source_target_pairs={{0,224},{32,0},{64,32},{96,64},{128,96},{160,128},{192,160},{224,1... | collective-permute-start | bytes 786440 | tf_op jit(solution)/shard_map/ppermute | solution.py:37
  230.4 17.1 %collective-permute-start.22 = (f32[256,512]{1,0:T(8,128)S(1)}, f32[256,512]{1,0:T(8,128)S(1)}, u32[]{:S(2)}, u32[]{:S(2)}) collective-permute-start(f32[256,512]{1,0:T(8,128)S(1)} %bitcast_add_fusion.4), channel_id=1, source_target_pairs={{0,8},{8,16},{16,24},{24,0},{1,9},{9,17},{17,25},{25,1},{2,10},{10... | collective-permute-start | bytes 1572872 | tf_op jit(solution)/shard_map/ppermute | solution.py:37
  234.8 8.7 %collective-permute-start.4 = (f32[128,512]{1,0:T(8,128)S(1)}, f32[128,512]{1,0:T(8,128)S(1)}, u32[]{:S(2)}, u32[]{:S(2)}) collective-permute-start(f32[128,512]{1,0:T(8,128)S(1)} %bitcast_add_fusion.16), channel_id=1, source_target_pairs={{0,32},{32,64},{64,96},{96,128},{128,160},{160,192},{192,224},{224... | collective-permute-start | bytes 786440 | tf_op jit(solution)/shard_map/ppermute | solution.py:37
  234.9 8.8 %collective-permute-start.14 = (f32[128,512]{1,0:T(8,128)S(1)}, f32[128,512]{1,0:T(8,128)S(1)}, u32[]{:S(2)}, u32[]{:S(2)}) collective-permute-start(f32[128,512]{1,0:T(8,128)S(1)} %bitcast_add_fusion.9), channel_id=1, source_target_pairs={{0,224},{32,0},{64,32},{96,64},{128,96},{160,128},{192,160},{224,1... | collective-permute-start | bytes 786440 | tf_op jit(solution)/shard_map/ppermute | solution.py:37
  238.6 9.3 %collective-permute-start.32 = (f32[256,512]{1,0:T(8,128)S(1)}, f32[256,512]{1,0:T(8,128)S(1)}, u32[]{:S(2)}, u32[]{:S(2)}) collective-permute-start(f32[256,512]{1,0:T(8,128)S(1)} %bitcast_add_fusion.1), channel_id=1, source_target_pairs={{0,24},{8,0},{16,8},{24,16},{1,25},{9,1},{17,9},{25,17},{2,26},{10... | collective-permute-start | bytes 1572872 | tf_op jit(solution)/shard_map/ppermute | solution.py:37
  243.6 9.9 %collective-permute-start.5 = (f32[128,512]{1,0:T(8,128)S(1)}, f32[128,512]{1,0:T(8,128)S(1)}, u32[]{:S(2)}, u32[]{:S(2)}) collective-permute-start(f32[128,512]{1,0:T(8,128)S(1)} %bitcast_add_fusion.15), channel_id=1, source_target_pairs={{0,32},{32,64},{64,96},{96,128},{128,160},{160,192},{192,224},{224... | collective-permute-start | bytes 786440 | tf_op jit(solution)/shard_map/ppermute | solution.py:37
  243.8 10.2 %collective-permute-start.15 = (f32[128,512]{1,0:T(8,128)S(1)}, f32[128,512]{1,0:T(8,128)S(1)}, u32[]{:S(2)}, u32[]{:S(2)}) collective-permute-start(f32[128,512]{1,0:T(8,128)S(1)} %bitcast_add_fusion.8), channel_id=1, source_target_pairs={{0,224},{32,0},{64,32},{96,64},{128,96},{160,128},{192,160},{224,1... | collective-permute-start | bytes 786440 | tf_op jit(solution)/shard_map/ppermute | solution.py:37
  247.7 10.1 %collective-permute-start.23 = (f32[32,512]{1,0:T(8,128)S(1)}, f32[32,512]{1,0:T(8,128)S(1)}, u32[]{:S(2)}, u32[]{:S(2)}) collective-permute-start(f32[32,512]{1,0:T(8,128)S(1)} %dynamic-slice_bitcast_fusion.5), channel_id=1, source_target_pairs={{0,32},{32,64},{64,96},{96,128},{128,160},{160,192},{192,224},{224... | collective-permute-start | bytes 196616 | tf_op jit(solution)/shard_map/ppermute | solution.py:37
  248.0 9.9 %collective-permute-start.33 = (f32[32,512]{1,0:T(8,128)S(1)}, f32[32,512]{1,0:T(8,128)S(1)}, u32[]{:S(2)}, u32[]{:S(2)}) collective-permute-start(f32[32,512]{1,0:T(8,128)S(1)} %dynamic-slice_bitcast_fusion.4), channel_id=1, source_target_pairs={{0,224},{32,0},{64,32},{96,64},{128,96},{160,128},{192,160},{224,1... | collective-permute-start | bytes 196616 | tf_op jit(solution)/shard_map/ppermute | solution.py:37
  253.5 24.7 %collective-permute-start.6 = (f32[128,512]{1,0:T(8,128)S(1)}, f32[128,512]{1,0:T(8,128)S(1)}, u32[]{:S(2)}, u32[]{:S(2)}) collective-permute-start(f32[128,512]{1,0:T(8,128)S(1)} %bitcast_add_fusion.14), channel_id=1, source_target_pairs={{0,32},{32,64},{64,96},{96,128},{128,160},{160,192},{192,224},{224... | collective-permute-start | bytes 786440 | tf_op jit(solution)/shard_map/ppermute | solution.py:37
  254.0 26.3 %collective-permute-start.16 = (f32[128,512]{1,0:T(8,128)S(1)}, f32[128,512]{1,0:T(8,128)S(1)}, u32[]{:S(2)}, u32[]{:S(2)}) collective-permute-start(f32[128,512]{1,0:T(8,128)S(1)} %bitcast_add_fusion.7), channel_id=1, source_target_pairs={{0,224},{32,0},{64,32},{96,64},{128,96},{160,128},{192,160},{224,1... | collective-permute-start | bytes 786440 | tf_op jit(solution)/shard_map/ppermute | solution.py:37
  274.5 7.2 %collective-permute-start.27 = (f32[32,512]{1,0:T(8,128)S(1)}, f32[32,512]{1,0:T(8,128)S(1)}, u32[]{:S(2)}, u32[]{:S(2)}) collective-permute-start(f32[32,512]{1,0:T(8,128)S(1)} %bitcast_add_fusion.30), channel_id=1, source_target_pairs={{0,32},{32,64},{64,96},{96,128},{128,160},{160,192},{192,224},{224... | collective-permute-start | bytes 196616 | tf_op jit(solution)/shard_map/ppermute | solution.py:37
  274.6 7.2 %collective-permute-start.37 = (f32[32,512]{1,0:T(8,128)S(1)}, f32[32,512]{1,0:T(8,128)S(1)}, u32[]{:S(2)}, u32[]{:S(2)}) collective-permute-start(f32[32,512]{1,0:T(8,128)S(1)} %bitcast_add_fusion.23), channel_id=1, source_target_pairs={{0,224},{32,0},{64,32},{96,64},{128,96},{160,128},{192,160},{224,1... | collective-permute-start | bytes 196616 | tf_op jit(solution)/shard_map/ppermute | solution.py:37
  278.2 6.9 %collective-permute-start.7 = (f32[32,512]{1,0:T(8,128)S(1)}, f32[32,512]{1,0:T(8,128)S(1)}, u32[]{:S(2)}, u32[]{:S(2)}) collective-permute-start(f32[32,512]{1,0:T(8,128)S(1)} %dynamic-slice_bitcast_fusion.7), channel_id=1, source_target_pairs={{0,8},{8,16},{16,24},{24,0},{1,9},{9,17},{17,25},{25,1},{2,10},{10... | collective-permute-start | bytes 196616 | tf_op jit(solution)/shard_map/ppermute | solution.py:37
  281.7 6.8 %collective-permute-start.28 = (f32[32,512]{1,0:T(8,128)S(1)}, f32[32,512]{1,0:T(8,128)S(1)}, u32[]{:S(2)}, u32[]{:S(2)}) collective-permute-start(f32[32,512]{1,0:T(8,128)S(1)} %bitcast_add_fusion.29), channel_id=1, source_target_pairs={{0,32},{32,64},{64,96},{96,128},{128,160},{160,192},{192,224},{224... | collective-permute-start | bytes 196616 | tf_op jit(solution)/shard_map/ppermute | solution.py:37
  281.8 6.8 %collective-permute-start.38 = (f32[32,512]{1,0:T(8,128)S(1)}, f32[32,512]{1,0:T(8,128)S(1)}, u32[]{:S(2)}, u32[]{:S(2)}) collective-permute-start(f32[32,512]{1,0:T(8,128)S(1)} %bitcast_add_fusion.22), channel_id=1, source_target_pairs={{0,224},{32,0},{64,32},{96,64},{128,96},{160,128},{192,160},{224,1... | collective-permute-start | bytes 196616 | tf_op jit(solution)/shard_map/ppermute | solution.py:37
  285.1 6.8 %collective-permute-start.8 = (f32[32,512]{1,0:T(8,128)S(1)}, f32[32,512]{1,0:T(8,128)S(1)}, u32[]{:S(2)}, u32[]{:S(2)}) collective-permute-start(f32[32,512]{1,0:T(8,128)S(1)} %bitcast_add_fusion.39), channel_id=1, source_target_pairs={{0,8},{8,16},{16,24},{24,0},{1,9},{9,17},{17,25},{25,1},{2,10},{10... | collective-permute-start | bytes 196616 | tf_op jit(solution)/shard_map/ppermute | solution.py:37
  288.6 6.8 %collective-permute-start.29 = (f32[32,512]{1,0:T(8,128)S(1)}, f32[32,512]{1,0:T(8,128)S(1)}, u32[]{:S(2)}, u32[]{:S(2)}) collective-permute-start(f32[32,512]{1,0:T(8,128)S(1)} %bitcast_add_fusion.28), channel_id=1, source_target_pairs={{0,32},{32,64},{64,96},{96,128},{128,160},{160,192},{192,224},{224... | collective-permute-start | bytes 196616 | tf_op jit(solution)/shard_map/ppermute | solution.py:37
  (19 other events, 126.4 us)
Sparse Core Ops, SparseCore 0:
  22.3 57.7 all-gather.1
  90.8 41.6 reduce-scatter.1

commit v3 on v2

--- a/solution.py
+++ b/solution.py
@@ -39,18 +39,12 @@
 
 
 def row_reduce(x, nz, nx):
-    rows, w = x.shape
-    c = rows // (nz * nx)
-    q = w // 4
+    q = x.shape[1] // 2
     outs = []
-    for j in range(4):
+    for j, d in enumerate((1, -1)):
         p = x[:, j * q:(j + 1) * q]
-        d = 1 if j % 2 == 0 else -1
-        if j < 2:
-            outs.append(ring_rs(ring_rs(p, "z", nz, d), "x", nx, d))
-        else:
-            p = p.reshape(nz, nx, c, q).transpose(1, 0, 2, 3).reshape(rows, q)
-            outs.append(ring_rs(ring_rs(p, "x", nx, d), "z", nz, d))
+        p = ring_rs(p, "z", nz, d)
+        outs.append(ring_rs(p, "x", nx, d))
     return jnp.concatenate(outs, axis=1)
 
 
@@ -129,5 +123,7 @@
     a, w = P(ROW, COL), P(COL, ROW)
     in_specs = (a, a, w, w, a, w, w, a)
     out_specs = (a, a, w, w, a)
-    body = lambda *args: shards(nz, nx, ny, nc, *args)
+    def body(*args):
+        return shards(nz, nx, ny, nc, *args)
+
     return jax.shard_map(body, mesh=m4, in_specs=in_specs, out_specs=out_specs, check_vma=False)

time: 311 us -> 316 us (1.016); the launches traced: 305 us -> 315 us
  starting transfers between devices: 82.3 us -> 42 us
  waiting for transfers between devices: 156 us -> 181 us
  other arithmetic: 15.2 us -> 36.9 us
    ppermute x40 -> x20, starting transfers between devices: 76.2 us -> 35.9 us  [ring_rs(): acc = lax.ppermute(acc, axis, perm) + own]
    ppermute x40 -> x20, waiting for transfers between devices: 24.1 us -> 49.9 us  [ring_rs(): acc = lax.ppermute(acc, axis, perm) + own]
    add x36 -> x18, other arithmetic: 1.35 us -> 21.9 us  [ring_rs(): acc = lax.ppermute(acc, axis, perm) + own]
  transfers between devices with their start and end apart: 43 -> 23, of which waited for: 15 -> 20; matrix products, arithmetic and copies ran while one was open for 5% -> 13% of each run, Pallas kernels for 0% -> 0%
where the time goes in v3:
time: 316 us; the launch traced here: 315 us
  waiting for transfers between devices  181 us (57%)
  starting transfers between devices  42 us (13%)
  other arithmetic  36.9 us (12%)
  matrix products  18 us (6%)
  between operations  14.3 us (5%)
  blocking collectives  13.9 us (4%)
  local copies, waits for them, and re-layouts  8.98 us (3%)
    all_gather x1, waiting for transfers between devices, shards(): lax.all_gather(lax.all_gather(local, 'x', axis=0, tiled=True), 'z', axis=...  51.9 us
    ppermute x20, waiting for transfers between devices, ring_rs(): acc = lax.ppermute(acc, axis, perm) + own  49.9 us
    reduce_scatter x1, waiting for transfers between devices, shards(): lax.psum_scatter(jnp.concatenate([joint_part, hidden_part], axis=1), COL,...  41.8 us
    all_to_all x1, waiting for transfers between devices, gather_rows(): return lax.all_to_all(tiled, axis, 0, 0, tiled=True)  37 us
    ppermute x20, starting transfers between devices, ring_rs(): acc = lax.ppermute(acc, axis, perm) + own  35.9 us
    add x18, other arithmetic, ring_rs(): acc = lax.ppermute(acc, axis, perm) + own  21.9 us
    all_gather x1, blocking collectives, shards(): lax.all_gather(local, 'x', axis=0, tiled=True)  13.9 us
  transfers between devices with their start and end apart: 23, of which 20 were waited for; matrix products, arithmetic and copies ran while one was open for 13% of the time, Pallas kernels for 0%

profile of v3, /device:TPU:8, one launch (start us, length us, event | category | flops | bytes accessed | tf_op | source)
XLA Modules:
  0.0 314.8 jit_solution(15914064517106453910)
XLA Ops:
  8.2 13.9 %all_gather.6 = bf16[128,2048]{1,0:T(8,128)(2,1)} all-gather(bf16[32,2048]{1,0:T(8,128)(2,1)S(1)} %pad_maximum_fusion.5), channel_id=1, replica_groups=mesh['z'=8,'x'=4,'y'=4,'core'=2] {'x'}, dimensions={0}, use_global_device_ids=true | all-gather | bytes 655360 | tf_op jit(solution)/shard_map/all_gather | solution.py:55
  25.3 2.8 bitcast_multiply_fusion.4
  28.1 51.9 %all-gather.2.cloned.1.call-done = bf16[1024,2048]{1,0:T(8,128)(2,1)} async-done(((bf16[128,2048]{1,0:T(8,128)(2,1)}), bf16[1024,2048]{1,0:T(8,128)(2,1)}) %all-gather.2.cloned.1.call-update) | async-done | bytes 4194320 | tf_op jit(solution)/shard_map/all_gather | solution.py:55
  80.0 4.8 %fusion.9 = f32[1024,1024]{0,1:T(8,128)S(1)} fusion(bf16[1024,2048]{1,0:T(8,128)(2,1)} %all-gather.2.cloned.1.call-done, bf16[1024,512]{1,0:T(8,128)(2,1)} %get-tuple-element.16, bf16[1024,512]{1,0:T(8,128)(2,1)} %get-tuple-element.17), kind=kOutput, calls=%fused_computation.14 | convolution fusion | flops 2151677952 | bytes 8388608 | tf_op jit(solution)/shard_map/dot_general | solution.py:62
  87.3 3.3 %pad_maximum_fusion = f32[1024,1536]{0,1:T(8,128)} fusion(f32[1024,512]{0,1:T(8,128)S(1)} %fusion.6, f32[1024,1024]{0,1:T(8,128)S(1)} %fusion.9), kind=kLoop, calls=%fused_computation | loop fusion | flops 1572864 | bytes 12582912 | tf_op jit(solution)/shard_map/concatenate | solution.py:67
  90.6 41.8 %reduce-scatter.2.cloned.1.call-done = f32[128,1536]{0,1:T(8,128)} async-done(((f32[1024,1536]{0,1:T(8,128)}), f32[128,1536]{0,1:T(8,128)}) %reduce-scatter.2.cloned.1.call-update) | async-done | bytes 786448 | tf_op jit(solution)/shard_map/reduce_scatter | solution.py:66
  135.9 6.1 %all-to-all-start = ((bf16[8,128,1536]{2,1,0:T(8,128)(2,1)}), bf16[8,128,1536]{2,1,0:T(8,128)(2,1)S(1)}, u32[]{:S(2)}, u32[]{:S(2)}) async-start(bf16[8,128,1536]{2,1,0:T(8,128)(2,1)} %tile.2), calls=%async_computation.1 | async-start | bytes 6291456 | tf_op jit(solution)/shard_map/all_to_all | solution.py:26
  142.0 37.0 %all-to-all-done = bf16[8,128,1536]{2,1,0:T(8,128)(2,1)S(1)} async-done(((bf16[8,128,1536]{2,1,0:T(8,128)(2,1)}), bf16[8,128,1536]{2,1,0:T(8,128)(2,1)S(1)}, u32[]{:S(2)}, u32[]{:S(2)}) %all-to-all-start) | async-done | bytes 3145760 | tf_op jit(solution)/shard_map/all_to_all | solution.py:26
  178.9 3.9 %fusion.2 = f32[1024,1024]{1,0:T(8,128)S(1)} fusion(bf16[1024,1536]{1,0:T(8,128)(2,1)S(1)} %bitcast.91, bf16[1024,512]{1,0:T(8,128)(2,1)} %get-tuple-element.16, bf16[1024,512]{1,0:T(8,128)(2,1)} %get-tuple-element.17), kind=kOutput, calls=%fused_computation.7 | convolution fusion | flops 2151677952 | bytes 8388608 | tf_op jit(solution)/shard_map/dot_general | solution.py:84
  183.8 3.3 %collective-permute-start.10 = (f32[128,1024]{1,0:T(8,128)}, f32[128,1024]{1,0:T(8,128)}, u32[]{:S(2)}, u32[]{:S(2)}) collective-permute-start(f32[128,1024]{1,0:T(8,128)} %dynamic-slice_bitcast_fusion), channel_id=1, source_target_pairs={{0,224},{32,0},{64,32},{96,64},{128,96},{160,128},{192,160},{224,1... | collective-permute-start | bytes 1572872 | tf_op jit(solution)/shard_map/ppermute | solution.py:37
  191.7 6.7 %collective-permute-done.10 = f32[128,1024]{1,0:T(8,128)} collective-permute-done((f32[128,1024]{1,0:T(8,128)}, f32[128,1024]{1,0:T(8,128)}, u32[]{:S(2)}, u32[]{:S(2)}) %collective-permute-start.10) | collective-permute-done | bytes 524320 | tf_op jit(solution)/shard_map/ppermute | solution.py:37
  200.4 3.7 %collective-permute-start.11 = (f32[128,1024]{1,0:T(8,128)}, f32[128,1024]{1,0:T(8,128)}, u32[]{:S(2)}, u32[]{:S(2)}) collective-permute-start(f32[128,1024]{1,0:T(8,128)} %bitcast_add_fusion.6), channel_id=1, source_target_pairs={{0,224},{32,0},{64,32},{96,64},{128,96},{160,128},{192,160},{224,1... | collective-permute-start | bytes 1572872 | tf_op jit(solution)/shard_map/ppermute | solution.py:37
  205.9 2.1 bitcast_add_fusion.13
  207.9 6.5 %collective-permute-done.11 = f32[128,1024]{1,0:T(8,128)} collective-permute-done((f32[128,1024]{1,0:T(8,128)}, f32[128,1024]{1,0:T(8,128)}, u32[]{:S(2)}, u32[]{:S(2)}) %collective-permute-start.11) | collective-permute-done | bytes 524320 | tf_op jit(solution)/shard_map/ppermute | solution.py:37
  216.5 3.7 %collective-permute-start.12 = (f32[128,1024]{1,0:T(8,128)}, f32[128,1024]{1,0:T(8,128)}, u32[]{:S(2)}, u32[]{:S(2)}) collective-permute-start(f32[128,1024]{1,0:T(8,128)} %bitcast_add_fusion.5), channel_id=1, source_target_pairs={{0,224},{32,0},{64,32},{96,64},{128,96},{160,128},{192,160},{224,1... | collective-permute-start | bytes 1572872 | tf_op jit(solution)/shard_map/ppermute | solution.py:37
  221.7 2.1 bitcast_add_fusion.12
  223.8 5.9 %collective-permute-done.12 = f32[128,1024]{1,0:T(8,128)} collective-permute-done((f32[128,1024]{1,0:T(8,128)}, f32[128,1024]{1,0:T(8,128)}, u32[]{:S(2)}, u32[]{:S(2)}) %collective-permute-start.12) | collective-permute-done | bytes 524320 | tf_op jit(solution)/shard_map/ppermute | solution.py:37
  231.7 3.7 %collective-permute-start.13 = (f32[128,1024]{1,0:T(8,128)}, f32[128,1024]{1,0:T(8,128)}, u32[]{:S(2)}, u32[]{:S(2)}) collective-permute-start(f32[128,1024]{1,0:T(8,128)} %bitcast_add_fusion.4), channel_id=1, source_target_pairs={{0,224},{32,0},{64,32},{96,64},{128,96},{160,128},{192,160},{224,1... | collective-permute-start | bytes 1572872 | tf_op jit(solution)/shard_map/ppermute | solution.py:37
  236.7 2.1 bitcast_add_fusion.11
  238.9 5.2 %collective-permute-done.13 = f32[128,1024]{1,0:T(8,128)} collective-permute-done((f32[128,1024]{1,0:T(8,128)}, f32[128,1024]{1,0:T(8,128)}, u32[]{:S(2)}, u32[]{:S(2)}) %collective-permute-start.13) | collective-permute-done | bytes 524320 | tf_op jit(solution)/shard_map/ppermute | solution.py:37
  245.3 3.8 %collective-permute-start.14 = (f32[128,1024]{1,0:T(8,128)S(1)}, f32[128,1024]{1,0:T(8,128)S(1)}, u32[]{:S(2)}, u32[]{:S(2)}) collective-permute-start(f32[128,1024]{1,0:T(8,128)S(1)} %bitcast_add_fusion.3), channel_id=1, source_target_pairs={{0,224},{32,0},{64,32},{96,64},{128,96},{160,128},{192,160},{224,1... | collective-permute-start | bytes 1572872 | tf_op jit(solution)/shard_map/ppermute | solution.py:37
  252.1 4.0 %fusion = f32[1024,1024]{1,0:T(8,128)S(1)} fusion(bf16[1024,1536]{1,0:T(8,128)(2,1)S(1)} %bitcast.93, bf16[1024,2048]{1,0:T(8,128)(2,1)} %all-gather.2.cloned.1.call-done), kind=kOutput, calls=%fused_computation.5 | convolution fusion | flops 2147483648 | bytes 8388608 | tf_op jit(solution)/shard_map/dot_general | solution.py:90
  257.7 3.8 %collective-permute-start.15 = (f32[128,1024]{1,0:T(8,128)S(1)}, f32[128,1024]{1,0:T(8,128)S(1)}, u32[]{:S(2)}, u32[]{:S(2)}) collective-permute-start(f32[128,1024]{1,0:T(8,128)S(1)} %bitcast_add_fusion.2), channel_id=1, source_target_pairs={{0,224},{32,0},{64,32},{96,64},{128,96},{160,128},{192,160},{224,1... | collective-permute-start | bytes 1572872 | tf_op jit(solution)/shard_map/ppermute | solution.py:37
  264.9 3.1 bitcast_multiply_fusion.1
  270.3 3.4 %collective-permute-start.16 = (f32[128,1024]{1,0:T(8,128)S(1)}, f32[128,1024]{1,0:T(8,128)S(1)}, u32[]{:S(2)}, u32[]{:S(2)}) collective-permute-start(f32[128,1024]{1,0:T(8,128)S(1)} %bitcast_add_fusion.1), channel_id=1, source_target_pairs={{0,224},{32,0},{64,32},{96,64},{128,96},{160,128},{192,160},{224,1... | collective-permute-start | bytes 1572872 | tf_op jit(solution)/shard_map/ppermute | solution.py:37
  277.2 2.7 bitcast_multiply_fusion
  281.6 2.8 collective-permute-start.17
  284.4 3.0 collective-permute-done.6
  291.9 2.8 collective-permute-done.7
  295.5 2.7 collective-permute-start.19
  298.2 2.8 collective-permute-done.8
  301.8 5.5 %collective-permute-done.9 = f32[32,1024]{1,0:T(8,128)S(1)} collective-permute-done((f32[32,1024]{1,0:T(8,128)S(1)}, f32[32,1024]{1,0:T(8,128)S(1)}, u32[]{:S(2)}, u32[]{:S(2)}) %collective-permute-start.9) | collective-permute-done | bytes 131104 | tf_op jit(solution)/shard_map/ppermute | solution.py:37
  (87 shorter events, 49.9 us)
Async XLA Ops:
  7.2 18.1 %copy-start.6 = (bf16[1024,512]{1,0:T(8,128)(2,1)S(1)}, bf16[1024,512]{1,0:T(8,128)(2,1)}, u32[]{:S(2)}) copy-start(bf16[1024,512]{1,0:T(8,128)(2,1)} %param.11) | copy-start | bytes 3145732
  7.2 72.8 %all-gather.2.cloned.1.call-start = ((), (), s32[]{:S(2)}) async-start(), calls=%async_computation.2 | async-start | bytes 4718592 | tf_op jit(solution)/shard_map/all_gather | solution.py:55
  22.1 110.4 %reduce-scatter.2.cloned.1.call-start = ((), (), s32[]{:S(2)}) async-start(), calls=%async_computation.3 | async-start | bytes 7077888 | tf_op jit(solution)/shard_map/reduce_scatter | solution.py:66
  80.0 6.0 %copy-start.4 = (bf16[512,1024]{1,0:T(8,128)(2,1)S(1)}, bf16[512,1024]{1,0:T(8,128)(2,1)}, u32[]{:S(2)}) copy-start(bf16[512,1024]{1,0:T(8,128)(2,1)} %param.12) | copy-start | bytes 3145732
  80.0 6.0 %copy-start.7 = (bf16[1024,2048]{1,0:T(8,128)(2,1)S(1)}, bf16[1024,2048]{1,0:T(8,128)(2,1)}, u32[]{:S(2)}) copy-start(bf16[1024,2048]{1,0:T(8,128)(2,1)} %all-gather.2.cloned.1.call-done) | copy-start | bytes 12582916
  85.0 1.0 copy-start.1
  135.9 43.1 %all-to-all-start = ((bf16[8,128,1536]{2,1,0:T(8,128)(2,1)}), bf16[8,128,1536]{2,1,0:T(8,128)(2,1)S(1)}, u32[]{:S(2)}, u32[]{:S(2)}) async-start(bf16[8,128,1536]{2,1,0:T(8,128)(2,1)} %tile.2), calls=%async_computation.1 | async-start | bytes 6291456 | tf_op jit(solution)/shard_map/all_to_all | solution.py:26
  182.8 5.6 %copy-start.3 = (f32[1024,1024]{1,0:T(8,128)}, f32[1024,1024]{1,0:T(8,128)S(1)}, u32[]{:S(2)}) copy-start(f32[1024,1024]{1,0:T(8,128)S(1)} %fusion.2) | copy-start | bytes 12582916
  182.8 4.3 %copy-start.2 = (bf16[4,128,8,128]{3,2,1,0:T(8,128)(2,1)S(1)}, bf16[4,128,8,128]{3,2,1,0:T(8,128)(2,1)}, u32[]{:S(2)}) copy-start(bf16[4,128,8,128]{3,2,1,0:T(8,128)(2,1)} %copy-done.1) | copy-start | bytes 3145732
  182.9 4.3 %copy-start.5 = (bf16[512,1024]{1,0:T(8,128)(2,1)S(1)}, bf16[512,1024]{1,0:T(8,128)(2,1)}, u32[]{:S(2)}) copy-start(bf16[512,1024]{1,0:T(8,128)(2,1)} %param.12) | copy-start | bytes 3145732
  183.8 14.5 %collective-permute-start.10 = (f32[128,1024]{1,0:T(8,128)}, f32[128,1024]{1,0:T(8,128)}, u32[]{:S(2)}, u32[]{:S(2)}) collective-permute-start(f32[128,1024]{1,0:T(8,128)} %dynamic-slice_bitcast_fusion), channel_id=1, source_target_pairs={{0,224},{32,0},{64,32},{96,64},{128,96},{160,128},{192,160},{224,1... | collective-permute-start | bytes 1572872 | tf_op jit(solution)/shard_map/ppermute | solution.py:37
  188.4 2.0 copy-start
  191.3 14.6 %collective-permute-start = (f32[128,1024]{1,0:T(8,128)}, f32[128,1024]{1,0:T(8,128)}, u32[]{:S(2)}, u32[]{:S(2)}) collective-permute-start(f32[128,1024]{1,0:T(8,128)} %dynamic-slice_bitcast_fusion.1), channel_id=1, source_target_pairs={{0,32},{32,64},{64,96},{96,128},{128,160},{160,192},{192,224},{224... | collective-permute-start | bytes 1572872 | tf_op jit(solution)/shard_map/ppermute | solution.py:37
  200.4 14.0 %collective-permute-start.11 = (f32[128,1024]{1,0:T(8,128)}, f32[128,1024]{1,0:T(8,128)}, u32[]{:S(2)}, u32[]{:S(2)}) collective-permute-start(f32[128,1024]{1,0:T(8,128)} %bitcast_add_fusion.6), channel_id=1, source_target_pairs={{0,224},{32,0},{64,32},{96,64},{128,96},{160,128},{192,160},{224,1... | collective-permute-start | bytes 1572872 | tf_op jit(solution)/shard_map/ppermute | solution.py:37
  207.9 13.8 %collective-permute-start.1 = (f32[128,1024]{1,0:T(8,128)}, f32[128,1024]{1,0:T(8,128)}, u32[]{:S(2)}, u32[]{:S(2)}) collective-permute-start(f32[128,1024]{1,0:T(8,128)} %bitcast_add_fusion.13), channel_id=1, source_target_pairs={{0,32},{32,64},{64,96},{96,128},{128,160},{160,192},{192,224},{224... | collective-permute-start | bytes 1572872 | tf_op jit(solution)/shard_map/ppermute | solution.py:37
  216.5 13.2 %collective-permute-start.12 = (f32[128,1024]{1,0:T(8,128)}, f32[128,1024]{1,0:T(8,128)}, u32[]{:S(2)}, u32[]{:S(2)}) collective-permute-start(f32[128,1024]{1,0:T(8,128)} %bitcast_add_fusion.5), channel_id=1, source_target_pairs={{0,224},{32,0},{64,32},{96,64},{128,96},{160,128},{192,160},{224,1... | collective-permute-start | bytes 1572872 | tf_op jit(solution)/shard_map/ppermute | solution.py:37
  223.8 12.9 %collective-permute-start.2 = (f32[128,1024]{1,0:T(8,128)}, f32[128,1024]{1,0:T(8,128)}, u32[]{:S(2)}, u32[]{:S(2)}) collective-permute-start(f32[128,1024]{1,0:T(8,128)} %bitcast_add_fusion.12), channel_id=1, source_target_pairs={{0,32},{32,64},{64,96},{96,128},{128,160},{160,192},{192,224},{224... | collective-permute-start | bytes 1572872 | tf_op jit(solution)/shard_map/ppermute | solution.py:37
  231.7 12.3 %collective-permute-start.13 = (f32[128,1024]{1,0:T(8,128)}, f32[128,1024]{1,0:T(8,128)}, u32[]{:S(2)}, u32[]{:S(2)}) collective-permute-start(f32[128,1024]{1,0:T(8,128)} %bitcast_add_fusion.4), channel_id=1, source_target_pairs={{0,224},{32,0},{64,32},{96,64},{128,96},{160,128},{192,160},{224,1... | collective-permute-start | bytes 1572872 | tf_op jit(solution)/shard_map/ppermute | solution.py:37
  238.7 12.1 %collective-permute-start.3 = (f32[128,1024]{1,0:T(8,128)}, f32[128,1024]{1,0:T(8,128)}, u32[]{:S(2)}, u32[]{:S(2)}) collective-permute-start(f32[128,1024]{1,0:T(8,128)} %bitcast_add_fusion.11), channel_id=1, source_target_pairs={{0,32},{32,64},{64,96},{96,128},{128,160},{160,192},{192,224},{224... | collective-permute-start | bytes 1572872 | tf_op jit(solution)/shard_map/ppermute | solution.py:37
  245.3 11.2 %collective-permute-start.14 = (f32[128,1024]{1,0:T(8,128)S(1)}, f32[128,1024]{1,0:T(8,128)S(1)}, u32[]{:S(2)}, u32[]{:S(2)}) collective-permute-start(f32[128,1024]{1,0:T(8,128)S(1)} %bitcast_add_fusion.3), channel_id=1, source_target_pairs={{0,224},{32,0},{64,32},{96,64},{128,96},{160,128},{192,160},{224,1... | collective-permute-start | bytes 1572872 | tf_op jit(solution)/shard_map/ppermute | solution.py:37
  252.0 11.0 %collective-permute-start.4 = (f32[128,1024]{1,0:T(8,128)S(1)}, f32[128,1024]{1,0:T(8,128)S(1)}, u32[]{:S(2)}, u32[]{:S(2)}) collective-permute-start(f32[128,1024]{1,0:T(8,128)S(1)} %bitcast_add_fusion.10), channel_id=1, source_target_pairs={{0,32},{32,64},{64,96},{96,128},{128,160},{160,192},{192,224},{224... | collective-permute-start | bytes 1572872 | tf_op jit(solution)/shard_map/ppermute | solution.py:37
  257.7 11.2 %collective-permute-start.15 = (f32[128,1024]{1,0:T(8,128)S(1)}, f32[128,1024]{1,0:T(8,128)S(1)}, u32[]{:S(2)}, u32[]{:S(2)}) collective-permute-start(f32[128,1024]{1,0:T(8,128)S(1)} %bitcast_add_fusion.2), channel_id=1, source_target_pairs={{0,224},{32,0},{64,32},{96,64},{128,96},{160,128},{192,160},{224,1... | collective-permute-start | bytes 1572872 | tf_op jit(solution)/shard_map/ppermute | solution.py:37
  264.1 11.4 %collective-permute-start.5 = (f32[128,1024]{1,0:T(8,128)S(1)}, f32[128,1024]{1,0:T(8,128)S(1)}, u32[]{:S(2)}, u32[]{:S(2)}) collective-permute-start(f32[128,1024]{1,0:T(8,128)S(1)} %bitcast_add_fusion.9), channel_id=1, source_target_pairs={{0,32},{32,64},{64,96},{96,128},{128,160},{160,192},{192,224},{224... | collective-permute-start | bytes 1572872 | tf_op jit(solution)/shard_map/ppermute | solution.py:37
  268.0 9.2 %copy-start.8 = (bf16[1024,2048]{1,0:T(8,128)(2,1)S(1)}, bf16[1024,2048]{1,0:T(8,128)(2,1)}, u32[]{:S(2)}) copy-start(bf16[1024,2048]{1,0:T(8,128)(2,1)} %all-gather.2.cloned.1.call-done) | copy-start | bytes 12582916
  270.3 10.1 %collective-permute-start.16 = (f32[128,1024]{1,0:T(8,128)S(1)}, f32[128,1024]{1,0:T(8,128)S(1)}, u32[]{:S(2)}, u32[]{:S(2)}) collective-permute-start(f32[128,1024]{1,0:T(8,128)S(1)} %bitcast_add_fusion.1), channel_id=1, source_target_pairs={{0,224},{32,0},{64,32},{96,64},{128,96},{160,128},{192,160},{224,1... | collective-permute-start | bytes 1572872 | tf_op jit(solution)/shard_map/ppermute | solution.py:37
  276.7 10.7 %collective-permute-start.6 = (f32[128,1024]{1,0:T(8,128)S(1)}, f32[128,1024]{1,0:T(8,128)S(1)}, u32[]{:S(2)}, u32[]{:S(2)}) collective-permute-start(f32[128,1024]{1,0:T(8,128)S(1)} %bitcast_add_fusion.8), channel_id=1, source_target_pairs={{0,32},{32,64},{64,96},{96,128},{128,160},{160,192},{192,224},{224... | collective-permute-start | bytes 1572872 | tf_op jit(solution)/shard_map/ppermute | solution.py:37
  281.6 8.5 %collective-permute-start.17 = (f32[32,1024]{1,0:T(8,128)S(1)}, f32[32,1024]{1,0:T(8,128)S(1)}, u32[]{:S(2)}, u32[]{:S(2)}) collective-permute-start(f32[32,1024]{1,0:T(8,128)S(1)} %dynamic-slice_bitcast_fusion.2), channel_id=1, source_target_pairs={{0,24},{8,0},{16,8},{24,16},{1,25},{9,1},{17,9},{25,17},{2,26},{10... | collective-permute-start | bytes 393224 | tf_op jit(solution)/shard_map/ppermute | solution.py:37
  288.5 6.3 %collective-permute-start.7 = (f32[32,1024]{1,0:T(8,128)S(1)}, f32[32,1024]{1,0:T(8,128)S(1)}, u32[]{:S(2)}, u32[]{:S(2)}) collective-permute-start(f32[32,1024]{1,0:T(8,128)S(1)} %dynamic-slice_bitcast_fusion.3), channel_id=1, source_target_pairs={{0,8},{8,16},{16,24},{24,0},{1,9},{9,17},{17,25},{25,1},{2,10},{10... | collective-permute-start | bytes 393224 | tf_op jit(solution)/shard_map/ppermute | solution.py:37
  290.1 5.4 %collective-permute-start.18 = (f32[32,1024]{1,0:T(8,128)S(1)}, f32[32,1024]{1,0:T(8,128)S(1)}, u32[]{:S(2)}, u32[]{:S(2)}) collective-permute-start(f32[32,1024]{1,0:T(8,128)S(1)} %bitcast_add_fusion.16), channel_id=1, source_target_pairs={{0,24},{8,0},{16,8},{24,16},{1,25},{9,1},{17,9},{25,17},{2,26},{10... | collective-permute-start | bytes 393224 | tf_op jit(solution)/shard_map/ppermute | solution.py:37
  294.8 6.3 %collective-permute-start.8 = (f32[32,1024]{1,0:T(8,128)S(1)}, f32[32,1024]{1,0:T(8,128)S(1)}, u32[]{:S(2)}, u32[]{:S(2)}) collective-permute-start(f32[32,1024]{1,0:T(8,128)S(1)} %bitcast_add_fusion.19), channel_id=1, source_target_pairs={{0,8},{8,16},{16,24},{24,0},{1,9},{9,17},{17,25},{25,1},{2,10},{10... | collective-permute-start | bytes 393224 | tf_op jit(solution)/shard_map/ppermute | solution.py:37
  295.5 5.7 %collective-permute-start.19 = (f32[32,1024]{1,0:T(8,128)S(1)}, f32[32,1024]{1,0:T(8,128)S(1)}, u32[]{:S(2)}, u32[]{:S(2)}) collective-permute-start(f32[32,1024]{1,0:T(8,128)S(1)} %bitcast_add_fusion.15), channel_id=1, source_target_pairs={{0,24},{8,0},{16,8},{24,16},{1,25},{9,1},{17,9},{25,17},{2,26},{10... | collective-permute-start | bytes 393224 | tf_op jit(solution)/shard_map/ppermute | solution.py:37
  301.0 6.3 %collective-permute-start.9 = (f32[32,1024]{1,0:T(8,128)S(1)}, f32[32,1024]{1,0:T(8,128)S(1)}, u32[]{:S(2)}, u32[]{:S(2)}) collective-permute-start(f32[32,1024]{1,0:T(8,128)S(1)} %bitcast_add_fusion.18), channel_id=1, source_target_pairs={{0,8},{8,16},{16,24},{24,0},{1,9},{9,17},{17,25},{25,1},{2,10},{10... | collective-permute-start | bytes 393224 | tf_op jit(solution)/shard_map/ppermute | solution.py:37
Sparse Core Ops, SparseCore 0:
  22.2 57.7 all-gather.1
  90.8 41.6 reduce-scatter.1

commit v4 on v2

--- a/solution.py
+++ b/solution.py
@@ -26,32 +26,34 @@
     return lax.all_to_all(tiled, axis, 0, 0, tiled=True)
 
 
-def ring_rs(x, axis, n, d):
+def line_rs(x, axis, n):
     c = x.shape[0] // n
     i = lax.axis_index(axis)
     chunks = x.reshape((n, c) + x.shape[1:])
-    perm = [(j, (j + d) % n) for j in range(n)]
-    acc = lax.dynamic_index_in_dim(chunks, (i - d) % n, 0, keepdims=False)
-    for s in range(1, n):
-        own = lax.dynamic_index_in_dim(chunks, (i - d * (s + 1)) % n, 0, keepdims=False)
-        acc = lax.ppermute(acc, axis, perm) + own
-    return acc
+
+    def own(k):
+        return lax.dynamic_index_in_dim(chunks, k % n, 0, keepdims=False)
+
+    total = own(i)
+    for reach, d in ((n // 2, 1), (n - 1 - n // 2, -1)):
+        if reach == 0:
+            continue
+        perm = [(j, (j + d) % n) for j in range(n)]
+        acc = own(i + d * reach)
+        for s in range(2, reach + 1):
+            acc = lax.ppermute(acc, axis, perm) + own(i + d * (reach - s + 1))
+        total = total + lax.ppermute(acc, axis, perm)
+    return total
 
 
 def row_reduce(x, nz, nx):
     rows, w = x.shape
     c = rows // (nz * nx)
-    q = w // 4
-    outs = []
-    for j in range(4):
-        p = x[:, j * q:(j + 1) * q]
-        d = 1 if j % 2 == 0 else -1
-        if j < 2:
-            outs.append(ring_rs(ring_rs(p, "z", nz, d), "x", nx, d))
-        else:
-            p = p.reshape(nz, nx, c, q).transpose(1, 0, 2, 3).reshape(rows, q)
-            outs.append(ring_rs(ring_rs(p, "x", nx, d), "z", nz, d))
-    return jnp.concatenate(outs, axis=1)
+    q = w // 2
+    first = line_rs(line_rs(x[:, :q], "z", nz), "x", nx)
+    p = x[:, q:].reshape(nz, nx, c, q).transpose(1, 0, 2, 3).reshape(rows, q)
+    second = line_rs(line_rs(p, "x", nx), "z", nz)
+    return jnp.concatenate([first, second], axis=1)
 
 
 def shards(nz, nx, ny, nc, tokens, cotangent, gate_weight, up_weight, down_weight, gate_mask, up_mask, down_mask):

time: 311 us -> 285 us (0.916); the launches traced: 305 us -> 283 us
  starting transfers between devices: 82.3 us -> 35.9 us
  waiting for transfers between devices: 156 us -> 167 us
  other arithmetic: 15.2 us -> 24.4 us
  local copies, waits for them, and re-layouts: 6.68 us -> 10.5 us
    ppermute x40 -> x20, starting transfers between devices: 76.2 us -> 29.8 us  [the longest x12 16.8 us: line_rs(): acc = lax.ppermute(acc, axis, perm) + own(i + d * (reach - s + 1))]
    ppermute x40 -> x20, waiting for transfers between devices: 24.1 us -> 36.5 us  [the longest x12 33.9 us: line_rs(): acc = lax.ppermute(acc, axis, perm) + own(i + d * (reach - s + 1))]
    add x36 -> x10, other arithmetic: 1.35 us -> 9.49 us  [the longest x8 6.85 us: line_rs(): acc = lax.ppermute(acc, axis, perm) + own(i + d * (reach - s + 1))]
  transfers between devices with their start and end apart: 43 -> 23, of which waited for: 15 -> 11; matrix products, arithmetic and copies ran while one was open for 5% -> 10% of each run, Pallas kernels for 0% -> 0%
where the time goes in v4:
time: 285 us; the launch traced here: 283 us
  waiting for transfers between devices  167 us (59%)
  starting transfers between devices  35.9 us (13%)
  other arithmetic  24.4 us (9%)
  matrix products  16.4 us (6%)
  between operations  14.3 us (5%)
  blocking collectives  13.9 us (5%)
  local copies, waits for them, and re-layouts  10.5 us (4%)
    all_gather x1, waiting for transfers between devices, shards(): lax.all_gather(lax.all_gather(local, 'x', axis=0, tiled=True), 'z', axis=...  51.9 us
    reduce_scatter x1, waiting for transfers between devices, shards(): lax.psum_scatter(jnp.concatenate([joint_part, hidden_part], axis=1), COL,...  41.8 us
    all_to_all x1, waiting for transfers between devices, gather_rows(): return lax.all_to_all(tiled, axis, 0, 0, tiled=True)  37 us
    ppermute x12, waiting for transfers between devices, line_rs(): acc = lax.ppermute(acc, axis, perm) + own(i + d * (reach - s + 1))  33.9 us
    ppermute x12, starting transfers between devices, line_rs(): acc = lax.ppermute(acc, axis, perm) + own(i + d * (reach - s + 1))  16.8 us
    all_gather x1, blocking collectives, shards(): lax.all_gather(local, 'x', axis=0, tiled=True)  13.9 us
    ppermute x8, starting transfers between devices, line_rs(): total = total + lax.ppermute(acc, axis, perm)  12.9 us
    add x8, other arithmetic, line_rs(): acc = lax.ppermute(acc, axis, perm) + own(i + d * (reach - s + 1))  6.85 us
  transfers between devices with their start and end apart: 23, of which 11 were waited for; matrix products, arithmetic and copies ran while one was open for 10% of the time, Pallas kernels for 0%

profile of v4, /device:TPU:8, one launch (start us, length us, event | category | flops | bytes accessed | tf_op | source)
XLA Modules:
  0.0 282.7 jit_solution(12885570829539947099)
XLA Ops:
  8.2 13.9 %all_gather.6 = bf16[128,2048]{1,0:T(8,128)(2,1)} all-gather(bf16[32,2048]{1,0:T(8,128)(2,1)S(1)} %pad_maximum_fusion.5), channel_id=1, replica_groups=mesh['z'=8,'x'=4,'y'=4,'core'=2] {'x'}, dimensions={0}, use_global_device_ids=true | all-gather | bytes 655360 | tf_op jit(solution)/shard_map/all_gather | solution.py:63
  25.3 2.8 bitcast_multiply_fusion.4
  28.1 51.9 %all-gather.2.cloned.1.call-done = bf16[1024,2048]{1,0:T(8,128)(2,1)} async-done(((bf16[128,2048]{1,0:T(8,128)(2,1)}), bf16[1024,2048]{1,0:T(8,128)(2,1)}) %all-gather.2.cloned.1.call-update) | async-done | bytes 4194320 | tf_op jit(solution)/shard_map/all_gather | solution.py:63
  80.0 4.8 %fusion.9 = f32[1024,1024]{0,1:T(8,128)S(1)} fusion(bf16[1024,2048]{1,0:T(8,128)(2,1)} %all-gather.2.cloned.1.call-done, bf16[1024,512]{1,0:T(8,128)(2,1)} %get-tuple-element.32, bf16[1024,512]{1,0:T(8,128)(2,1)} %get-tuple-element.33), kind=kOutput, calls=%fused_computation.14 | convolution fusion | flops 2151677952 | bytes 8388608 | tf_op jit(solution)/shard_map/dot_general | solution.py:70
  87.3 3.3 %pad_maximum_fusion = f32[1024,1536]{0,1:T(8,128)} fusion(f32[1024,512]{0,1:T(8,128)S(1)} %fusion.6, f32[1024,1024]{0,1:T(8,128)S(1)} %fusion.9), kind=kLoop, calls=%fused_computation | loop fusion | flops 1572864 | bytes 12582912 | tf_op jit(solution)/shard_map/concatenate | solution.py:75
  90.6 41.8 %reduce-scatter.2.cloned.1.call-done = f32[128,1536]{0,1:T(8,128)} async-done(((f32[1024,1536]{0,1:T(8,128)}), f32[128,1536]{0,1:T(8,128)}) %reduce-scatter.2.cloned.1.call-update) | async-done | bytes 786448 | tf_op jit(solution)/shard_map/reduce_scatter | solution.py:74
  133.9 1.9 tile.2
  135.8 6.1 %all-to-all-start = ((bf16[8,128,1536]{2,1,0:T(8,128)(2,1)}), bf16[8,128,1536]{2,1,0:T(8,128)(2,1)S(1)}, u32[]{:S(2)}, u32[]{:S(2)}) async-start(bf16[8,128,1536]{2,1,0:T(8,128)(2,1)} %tile.2), calls=%async_computation.1 | async-start | bytes 6291456 | tf_op jit(solution)/shard_map/all_to_all | solution.py:26
  141.9 37.0 %all-to-all-done = bf16[8,128,1536]{2,1,0:T(8,128)(2,1)S(1)} async-done(((bf16[8,128,1536]{2,1,0:T(8,128)(2,1)}), bf16[8,128,1536]{2,1,0:T(8,128)(2,1)S(1)}, u32[]{:S(2)}, u32[]{:S(2)}) %all-to-all-start) | async-done | bytes 3145760 | tf_op jit(solution)/shard_map/all_to_all | solution.py:26
  178.9 3.9 %fusion.2 = f32[1024,1024]{1,0:T(8,128)S(1)} fusion(bf16[1024,1536]{1,0:T(8,128)(2,1)S(1)} %bitcast.105, bf16[1024,512]{1,0:T(8,128)(2,1)} %get-tuple-element.32, bf16[1024,512]{1,0:T(8,128)(2,1)} %get-tuple-element.33), kind=kOutput, calls=%fused_computation.7 | convolution fusion | flops 2151677952 | bytes 8388608 | tf_op jit(solution)/shard_map/dot_general | solution.py:92
  187.8 2.1 copy-done
  192.5 1.8 collective-permute-start.4
  194.3 11.9 %collective-permute-done = f32[128,1024]{1,0:T(8,128)} collective-permute-done((f32[128,1024]{1,0:T(8,128)}, f32[128,1024]{1,0:T(8,128)}, u32[]{:S(2)}, u32[]{:S(2)}) %collective-permute-start) | collective-permute-done | bytes 524320 | tf_op jit(solution)/shard_map/ppermute | solution.py:44
  206.2 2.1 bitcast_add_fusion.6
  208.4 2.7 collective-permute-start.12
  211.1 1.7 bitcast_add_fusion
  213.1 9.5 %collective-permute-done.1 = f32[128,1024]{1,0:T(8,128)} collective-permute-done((f32[128,1024]{1,0:T(8,128)}, f32[128,1024]{1,0:T(8,128)}, u32[]{:S(2)}, u32[]{:S(2)}) %collective-permute-start.1) | collective-permute-done | bytes 524320 | tf_op jit(solution)/shard_map/ppermute | solution.py:44
  224.3 3.2 %collective-permute-start.5 = (f32[128,1024]{1,0:T(8,128)S(1)}, f32[128,1024]{1,0:T(8,128)S(1)}, u32[]{:S(2)}, u32[]{:S(2)}) collective-permute-start(f32[128,1024]{1,0:T(8,128)S(1)} %get-tuple-element.12), channel_id=1, source_target_pairs={{0,224},{32,0},{64,32},{96,64},{128,96},{160,128},{192,160},{224,1... | collective-permute-start | bytes 1572872 | tf_op jit(solution)/shard_map/ppermute | solution.py:44
  227.6 2.4 fusion
  230.7 3.0 %bitcast_multiply_fusion.1 = (f32[1024,512]{1,0:T(8,128)}, f32[1024,512]{1,0:T(8,128)}) fusion(f32[128,8,4,128]{3,2,1,0:T(4,128)S(1)} %bitcast.104, f32[1024,1024]{1,0:T(8,128)S(1)} %fusion, f32[128,8,4,128]{3,2,1,0:T(4,128)S(1)} %bitcast.103), kind=kLoop, calls=%fused_computation.2 | loop fusion | flops 1048576 | bytes 12582912 | tf_op jit(solution)/shard_map/mul | solution.py:20
  233.7 3.8 %collective-permute-done.2 = f32[128,1024]{1,0:T(8,128)S(1)} collective-permute-done((f32[128,1024]{1,0:T(8,128)S(1)}, f32[128,1024]{1,0:T(8,128)S(1)}, u32[]{:S(2)}, u32[]{:S(2)}) %collective-permute-start.2) | collective-permute-done | bytes 524320 | tf_op jit(solution)/shard_map/ppermute | solution.py:44
  238.9 3.2 %collective-permute-start.6 = (f32[128,1024]{1,0:T(8,128)S(1)}, f32[128,1024]{1,0:T(8,128)S(1)}, u32[]{:S(2)}, u32[]{:S(2)}) collective-permute-start(f32[128,1024]{1,0:T(8,128)S(1)} %get-tuple-element.10), channel_id=1, source_target_pairs={{0,224},{32,0},{64,32},{96,64},{128,96},{160,128},{192,160},{224,1... | collective-permute-start | bytes 1572872 | tf_op jit(solution)/shard_map/ppermute | solution.py:45
  244.0 2.7 bitcast_multiply_fusion
  246.7 3.2 %collective-permute-start.17 = (f32[32,1024]{1,0:T(8,128)S(1)}, f32[32,1024]{1,0:T(8,128)S(1)}, u32[]{:S(2)}, u32[]{:S(2)}) collective-permute-start(f32[32,1024]{1,0:T(8,128)S(1)} %get-tuple-element.20), channel_id=1, source_target_pairs={{0,224},{32,0},{64,32},{96,64},{128,96},{160,128},{192,160},{224,1... | collective-permute-start | bytes 393224 | tf_op jit(solution)/shard_map/ppermute | solution.py:44
  249.9 4.1 %collective-permute-done.13 = f32[32,1024]{1,0:T(8,128)S(1)} collective-permute-done((f32[32,1024]{1,0:T(8,128)S(1)}, f32[32,1024]{1,0:T(8,128)S(1)}, u32[]{:S(2)}, u32[]{:S(2)}) %collective-permute-start.13) | collective-permute-done | bytes 131104 | tf_op jit(solution)/shard_map/ppermute | solution.py:44
  257.3 1.8 collective-permute-start.9
  259.1 2.0 collective-permute-done.14
  262.1 2.4 collective-permute-start.18
  266.0 2.5 collective-permute-done.15
  268.6 1.7 collective-permute-start.16
  270.2 1.7 collective-permute-start.19
  272.6 2.3 collective-permute-done.16
  (80 shorter events, 29.5 us)
Async XLA Ops:
  7.2 18.1 %copy-start.6 = (bf16[1024,512]{1,0:T(8,128)(2,1)S(1)}, bf16[1024,512]{1,0:T(8,128)(2,1)}, u32[]{:S(2)}) copy-start(bf16[1024,512]{1,0:T(8,128)(2,1)} %param.11) | copy-start | bytes 3145732
  7.2 72.8 %all-gather.2.cloned.1.call-start = ((), (), s32[]{:S(2)}) async-start(), calls=%async_computation.2 | async-start | bytes 4718592 | tf_op jit(solution)/shard_map/all_gather | solution.py:63
  22.1 110.4 %reduce-scatter.2.cloned.1.call-start = ((), (), s32[]{:S(2)}) async-start(), calls=%async_computation.3 | async-start | bytes 7077888 | tf_op jit(solution)/shard_map/reduce_scatter | solution.py:74
  80.0 6.0 %copy-start.4 = (bf16[512,1024]{1,0:T(8,128)(2,1)S(1)}, bf16[512,1024]{1,0:T(8,128)(2,1)}, u32[]{:S(2)}) copy-start(bf16[512,1024]{1,0:T(8,128)(2,1)} %param.12) | copy-start | bytes 3145732
  80.0 6.0 %copy-start.7 = (bf16[1024,2048]{1,0:T(8,128)(2,1)S(1)}, bf16[1024,2048]{1,0:T(8,128)(2,1)}, u32[]{:S(2)}) copy-start(bf16[1024,2048]{1,0:T(8,128)(2,1)} %all-gather.2.cloned.1.call-done) | copy-start | bytes 12582916
  85.0 1.0 copy-start.2
  135.8 43.1 %all-to-all-start = ((bf16[8,128,1536]{2,1,0:T(8,128)(2,1)}), bf16[8,128,1536]{2,1,0:T(8,128)(2,1)S(1)}, u32[]{:S(2)}, u32[]{:S(2)}) async-start(bf16[8,128,1536]{2,1,0:T(8,128)(2,1)} %tile.2), calls=%async_computation.1 | async-start | bytes 6291456 | tf_op jit(solution)/shard_map/all_to_all | solution.py:26
  183.5 4.3 %copy-start.1 = (f32[8,4,32,1024]{3,2,0,1:T(8,128)}, f32[8,4,32,1024]{3,2,0,1:T(8,128)S(1)}, u32[]{:S(2)}) copy-start(f32[8,4,32,1024]{3,2,0,1:T(8,128)S(1)} %copy.21) | copy-start | bytes 12582916
  183.5 3.0 %copy-start.3 = (bf16[4,128,8,128]{3,2,1,0:T(8,128)(2,1)S(1)}, bf16[4,128,8,128]{3,2,1,0:T(8,128)(2,1)}, u32[]{:S(2)}) copy-start(bf16[4,128,8,128]{3,2,1,0:T(8,128)(2,1)} %copy-done.2) | copy-start | bytes 3145732
  183.5 3.0 %copy-start.5 = (bf16[512,1024]{1,0:T(8,128)(2,1)S(1)}, bf16[512,1024]{1,0:T(8,128)(2,1)}, u32[]{:S(2)}) copy-start(bf16[512,1024]{1,0:T(8,128)(2,1)} %param.12) | copy-start | bytes 3145732
  185.0 26.2 %collective-permute-start.10 = (f32[256,1024]{1,0:T(8,128)}, f32[256,1024]{1,0:T(8,128)}, u32[]{:S(2)}, u32[]{:S(2)}) collective-permute-start(f32[256,1024]{1,0:T(8,128)} %get-tuple-element.7), channel_id=1, source_target_pairs={{0,8},{8,16},{16,24},{24,0},{1,9},{9,17},{17,25},{25,1},{2,10},{10... | collective-permute-start | bytes 3145736 | tf_op jit(solution)/shard_map/ppermute | solution.py:44
  187.8 2.1 copy-start
  190.9 15.3 %collective-permute-start = (f32[128,1024]{1,0:T(8,128)}, f32[128,1024]{1,0:T(8,128)}, u32[]{:S(2)}, u32[]{:S(2)}) collective-permute-start(f32[128,1024]{1,0:T(8,128)} %get-tuple-element.13), channel_id=1, source_target_pairs={{0,32},{32,64},{64,96},{96,128},{128,160},{160,192},{192,224},{224... | collective-permute-start | bytes 1572872 | tf_op jit(solution)/shard_map/ppermute | solution.py:44
  192.5 20.6 %collective-permute-start.4 = (f32[128,1024]{1,0:T(8,128)}, f32[128,1024]{1,0:T(8,128)}, u32[]{:S(2)}, u32[]{:S(2)}) collective-permute-start(f32[128,1024]{1,0:T(8,128)} %get-tuple-element.14), channel_id=1, source_target_pairs={{0,224},{32,0},{64,32},{96,64},{128,96},{160,128},{192,160},{224,1... | collective-permute-start | bytes 1572872 | tf_op jit(solution)/shard_map/ppermute | solution.py:44
  208.3 14.3 %collective-permute-start.1 = (f32[128,1024]{1,0:T(8,128)}, f32[128,1024]{1,0:T(8,128)}, u32[]{:S(2)}, u32[]{:S(2)}) collective-permute-start(f32[128,1024]{1,0:T(8,128)} %bitcast_add_fusion.6), channel_id=1, source_target_pairs={{0,32},{32,64},{64,96},{96,128},{128,160},{160,192},{192,224},{224... | collective-permute-start | bytes 1572872 | tf_op jit(solution)/shard_map/ppermute | solution.py:44
  208.4 19.1 %copy-start.8 = (bf16[1024,2048]{1,0:T(8,128)(2,1)S(1)}, bf16[1024,2048]{1,0:T(8,128)(2,1)}, u32[]{:S(2)}) copy-start(bf16[1024,2048]{1,0:T(8,128)(2,1)} %all-gather.2.cloned.1.call-done) | copy-start | bytes 12582916
  208.4 33.7 %collective-permute-start.12 = (f32[256,1024]{1,0:T(8,128)}, f32[256,1024]{1,0:T(8,128)S(1)}, u32[]{:S(2)}, u32[]{:S(2)}) collective-permute-start(f32[256,1024]{1,0:T(8,128)} %get-tuple-element.8), channel_id=1, source_target_pairs={{0,24},{8,0},{16,8},{24,16},{1,25},{9,1},{17,9},{25,17},{2,26},{10... | collective-permute-start | bytes 3145736 | tf_op jit(solution)/shard_map/ppermute | solution.py:45
  212.8 29.4 %collective-permute-start.11 = (f32[256,1024]{1,0:T(8,128)S(1)}, f32[256,1024]{1,0:T(8,128)S(1)}, u32[]{:S(2)}, u32[]{:S(2)}) collective-permute-start(f32[256,1024]{1,0:T(8,128)S(1)} %bitcast_add_fusion), channel_id=1, source_target_pairs={{0,8},{8,16},{16,24},{24,0},{1,9},{9,17},{17,25},{25,1},{2,10},{10... | collective-permute-start | bytes 3145736 | tf_op jit(solution)/shard_map/ppermute | solution.py:45
  224.2 13.2 %collective-permute-start.2 = (f32[128,1024]{1,0:T(8,128)S(1)}, f32[128,1024]{1,0:T(8,128)S(1)}, u32[]{:S(2)}, u32[]{:S(2)}) collective-permute-start(f32[128,1024]{1,0:T(8,128)S(1)} %get-tuple-element.11), channel_id=1, source_target_pairs={{0,32},{32,64},{64,96},{96,128},{128,160},{160,192},{192,224},{224... | collective-permute-start | bytes 1572872 | tf_op jit(solution)/shard_map/ppermute | solution.py:44
  224.3 13.1 %collective-permute-start.5 = (f32[128,1024]{1,0:T(8,128)S(1)}, f32[128,1024]{1,0:T(8,128)S(1)}, u32[]{:S(2)}, u32[]{:S(2)}) collective-permute-start(f32[128,1024]{1,0:T(8,128)S(1)} %get-tuple-element.12), channel_id=1, source_target_pairs={{0,224},{32,0},{64,32},{96,64},{128,96},{160,128},{192,160},{224,1... | collective-permute-start | bytes 1572872 | tf_op jit(solution)/shard_map/ppermute | solution.py:44
  238.8 15.8 %collective-permute-start.3 = (f32[128,1024]{1,0:T(8,128)S(1)}, f32[128,1024]{1,0:T(8,128)S(1)}, u32[]{:S(2)}, u32[]{:S(2)}) collective-permute-start(f32[128,1024]{1,0:T(8,128)S(1)} %get-tuple-element.9), channel_id=1, source_target_pairs={{0,32},{32,64},{64,96},{96,128},{128,160},{160,192},{192,224},{224... | collective-permute-start | bytes 1572872 | tf_op jit(solution)/shard_map/ppermute | solution.py:45
  238.9 15.7 %collective-permute-start.6 = (f32[128,1024]{1,0:T(8,128)S(1)}, f32[128,1024]{1,0:T(8,128)S(1)}, u32[]{:S(2)}, u32[]{:S(2)}) collective-permute-start(f32[128,1024]{1,0:T(8,128)S(1)} %get-tuple-element.10), channel_id=1, source_target_pairs={{0,224},{32,0},{64,32},{96,64},{128,96},{160,128},{192,160},{224,1... | collective-permute-start | bytes 1572872 | tf_op jit(solution)/shard_map/ppermute | solution.py:45
  243.7 10.3 %collective-permute-start.13 = (f32[32,1024]{1,0:T(8,128)S(1)}, f32[32,1024]{1,0:T(8,128)S(1)}, u32[]{:S(2)}, u32[]{:S(2)}) collective-permute-start(f32[32,1024]{1,0:T(8,128)S(1)} %get-tuple-element.19), channel_id=1, source_target_pairs={{0,32},{32,64},{64,96},{96,128},{128,160},{160,192},{192,224},{224... | collective-permute-start | bytes 393224 | tf_op jit(solution)/shard_map/ppermute | solution.py:44
  246.7 12.4 %collective-permute-start.17 = (f32[32,1024]{1,0:T(8,128)S(1)}, f32[32,1024]{1,0:T(8,128)S(1)}, u32[]{:S(2)}, u32[]{:S(2)}) collective-permute-start(f32[32,1024]{1,0:T(8,128)S(1)} %get-tuple-element.20), channel_id=1, source_target_pairs={{0,224},{32,0},{64,32},{96,64},{128,96},{160,128},{192,160},{224,1... | collective-permute-start | bytes 393224 | tf_op jit(solution)/shard_map/ppermute | solution.py:44
  254.0 7.1 %collective-permute-start.14 = (f32[32,1024]{1,0:T(8,128)S(1)}, f32[32,1024]{1,0:T(8,128)S(1)}, u32[]{:S(2)}, u32[]{:S(2)}) collective-permute-start(f32[32,1024]{1,0:T(8,128)S(1)} %bitcast_add_fusion.12), channel_id=1, source_target_pairs={{0,32},{32,64},{64,96},{96,128},{128,160},{160,192},{192,224},{224... | collective-permute-start | bytes 393224 | tf_op jit(solution)/shard_map/ppermute | solution.py:44
  255.8 8.7 %collective-permute-start.7 = (f32[32,1024]{1,0:T(8,128)S(1)}, f32[32,1024]{1,0:T(8,128)S(1)}, u32[]{:S(2)}, u32[]{:S(2)}) collective-permute-start(f32[32,1024]{1,0:T(8,128)S(1)} %get-tuple-element.24), channel_id=1, source_target_pairs={{0,8},{8,16},{16,24},{24,0},{1,9},{9,17},{17,25},{25,1},{2,10},{10... | collective-permute-start | bytes 393224 | tf_op jit(solution)/shard_map/ppermute | solution.py:44
  257.3 14.6 %collective-permute-start.9 = (f32[32,1024]{1,0:T(8,128)S(1)}, f32[32,1024]{1,0:T(8,128)S(1)}, u32[]{:S(2)}, u32[]{:S(2)}) collective-permute-start(f32[32,1024]{1,0:T(8,128)S(1)} %get-tuple-element.25), channel_id=1, source_target_pairs={{0,24},{8,0},{16,8},{24,16},{1,25},{9,1},{17,9},{25,17},{2,26},{10... | collective-permute-start | bytes 393224 | tf_op jit(solution)/shard_map/ppermute | solution.py:45
  261.2 7.4 %collective-permute-start.15 = (f32[32,1024]{1,0:T(8,128)S(1)}, f32[32,1024]{1,0:T(8,128)S(1)}, u32[]{:S(2)}, u32[]{:S(2)}) collective-permute-start(f32[32,1024]{1,0:T(8,128)S(1)} %get-tuple-element.17), channel_id=1, source_target_pairs={{0,32},{32,64},{64,96},{96,128},{128,160},{160,192},{192,224},{224... | collective-permute-start | bytes 393224 | tf_op jit(solution)/shard_map/ppermute | solution.py:44
  262.1 6.4 %collective-permute-start.18 = (f32[32,1024]{1,0:T(8,128)S(1)}, f32[32,1024]{1,0:T(8,128)S(1)}, u32[]{:S(2)}, u32[]{:S(2)}) collective-permute-start(f32[32,1024]{1,0:T(8,128)S(1)} %get-tuple-element.18), channel_id=1, source_target_pairs={{0,224},{32,0},{64,32},{96,64},{128,96},{160,128},{192,160},{224,1... | collective-permute-start | bytes 393224 | tf_op jit(solution)/shard_map/ppermute | solution.py:44
  264.5 7.4 %collective-permute-start.8 = (f32[32,1024]{1,0:T(8,128)S(1)}, f32[32,1024]{1,0:T(8,128)S(1)}, u32[]{:S(2)}, u32[]{:S(2)}) collective-permute-start(f32[32,1024]{1,0:T(8,128)S(1)} %bitcast_add_fusion.14), channel_id=1, source_target_pairs={{0,8},{8,16},{16,24},{24,0},{1,9},{9,17},{17,25},{25,1},{2,10},{10... | collective-permute-start | bytes 393224 | tf_op jit(solution)/shard_map/ppermute | solution.py:45
  268.6 6.3 %collective-permute-start.16 = (f32[32,1024]{1,0:T(8,128)S(1)}, f32[32,1024]{1,0:T(8,128)S(1)}, u32[]{:S(2)}, u32[]{:S(2)}) collective-permute-start(f32[32,1024]{1,0:T(8,128)S(1)} %get-tuple-element.15), channel_id=1, source_target_pairs={{0,32},{32,64},{64,96},{96,128},{128,160},{160,192},{192,224},{224... | collective-permute-start | bytes 393224 | tf_op jit(solution)/shard_map/ppermute | solution.py:45
  270.2 5.0 %collective-permute-start.19 = (f32[32,1024]{1,0:T(8,128)S(1)}, f32[32,1024]{1,0:T(8,128)S(1)}, u32[]{:S(2)}, u32[]{:S(2)}) collective-permute-start(f32[32,1024]{1,0:T(8,128)S(1)} %get-tuple-element.16), channel_id=1, source_target_pairs={{0,224},{32,0},{64,32},{96,64},{128,96},{160,128},{192,160},{224,1... | collective-permute-start | bytes 393224 | tf_op jit(solution)/shard_map/ppermute | solution.py:45
Sparse Core Ops, SparseCore 0:
  22.2 57.7 all-gather.1
  90.7 41.6 reduce-scatter.1
